TPU v7x, 128 devices: a whole 4x4x4 slice. The times are simulated.
128 devices in a mesh: gx: 8 (over x, core), gy: 16 (over z, y).
Axes of the slice: x: 4, y: 4, z: 4, core: 2. Of those that a mesh axis runs over, the one named last changes fastest.
Arguments:
- start_disp: float32 [3, 256, 512, 128], P(None, 'gx', 'gy'), may hold values from -6 to 6
- start_vel: float32 [3, 256, 512, 128], P(None, 'gx', 'gy'), may hold values from -6 to 6
- stiffness: float32 [256, 512, 128], P('gx', 'gy'), may hold values from 0.5 to 2
- cell_mass: float32 [256, 512, 128], P('gx', 'gy'), may hold values from 0.5 to 2
- contact_cells: int32 [8, 16, 512], P('gx', 'gy'), may hold values from 0 to 1023
- contact_match: int32 [8, 16, 512], P('gx', 'gy'), may hold values from 0 to 511, each once within a row
- eroded_cells: int32 [8, 8, 16, 512], P(None, 'gx', 'gy'), may hold values from 0 to 131071
- owner_ids: int32 [8, 8, 16, 512, 1], P(None, 'gx', 'gy'), may hold values from 0 to 15; in each aligned block of 512 rows (0 to 511, 512 to 1023, ..., all dimensions but the last counted through in order) at most 128 rows name the same one
- bed_position: float32 [8, 16, 3, 2048], P('gx', 'gy'), may hold values from -6 to 6
- bed_velocity: float32 [8, 16, 3, 2048], P('gx', 'gy'), may hold values from -6 to 6
- bed_neighbours: int32 [8, 16, 8, 2048], P('gx', 'gy'), may hold values from 0 to 127
Outputs:
- final_disp: float32 [3, 256, 512, 128], P(None, 'gx', 'gy')
- final_vel: float32 [3, 256, 512, 128], P(None, 'gx', 'gy')
Inputs may be any that keep to these rules, and one draw needn't show every extreme that they name: `owner_ids`: in each step, at most 128 records of one block name one owner, and some block names some owner exactly 128 times.
All inputs are finite; a program needn't handle non-finite values.
Results may differ from a plain program's by a relative error of at most 0.0001.
Values sent between devices are 32-bit elements; how exact they have to be, the bound alone decides.
No kernel may reach another device: no remote copies, remote signals or barrier semaphores. Data moves between devices by JAX's collectives and lax.ppermute only.
A program may use at most 128 MiB of HBM per device.

v0:
```python
import jax
import jax.numpy as jnp
from jax import lax
from jax.sharding import PartitionSpec as P

TIME_STEP = 0.2
CONTACT_K = 0.5
PARTICLE_K = 1.0
DRAG_COEF = 0.5
HIGHEST = lax.Precision.HIGHEST


def padded_2(cells, sides, width):
    for axis, dim in sides:
        count = lax.axis_size(axis)
        ends = count - 1
        head = lax.slice_in_dim(cells, 0, width, axis=dim)
        tail = lax.slice_in_dim(cells, cells.shape[dim] - width, cells.shape[dim], axis=dim)
        cells = jnp.concatenate(
            [
                lax.ppermute(tail, axis, [(i, (i + 1) % count) for i in range(ends)]),
                cells,
                lax.ppermute(head, axis, [((i + 1) % count, i) for i in range(ends)]),
            ],
            axis=dim,
        )
    return cells


def from_partner(value, axis, stride):
    mask = 2**stride
    pairs = [(source, source ^ mask) for source in range(lax.axis_size(axis))]
    return lax.ppermute(value, axis, pairs)


def depth_sum(field):
    zeros = jnp.zeros_like(field[..., :1])
    upper = jnp.concatenate([field[..., 1:], zeros], axis=-1)
    lower = jnp.concatenate([zeros, field[..., :-1]], axis=-1)
    return upper + lower


def local(
    start_disp,
    start_vel,
    stiffness,
    cell_mass,
    contact_cells,
    contact_match,
    eroded_cells,
    owner_ids,
    bed_position,
    bed_velocity,
    bed_neighbours,
):
    cols_x = start_disp.shape[1]
    cols_y = start_disp.shape[2]
    layers = start_disp.shape[3]
    n_cols = cols_x * cols_y
    n_owner = lax.axis_size("gy")
    n_slots = bed_position.shape[3]
    capacity = n_slots // n_owner
    row_block = min(128, n_slots)
    n_blocks = n_slots // row_block
    n_nbr = bed_neighbours.shape[2]
    n_seg = contact_cells.shape[2]
    n_rec = eroded_cells.shape[3]
    col_range = jnp.arange(n_cols, dtype=jnp.int32)
    layer_range = jnp.arange(layers, dtype=jnp.int32)
    seg_hot = (contact_cells[0, 0][:, None] == col_range[None, :]).astype(jnp.float32)
    match_hot = (
        contact_match[0, 0][:, None] == jnp.arange(n_seg, dtype=jnp.int32)[None, :]
    ).astype(jnp.float32)
    local_nbr = bed_neighbours[0, 0].reshape(n_nbr, n_blocks, row_block).transpose(1, 0, 2)
    nbr_hot = (local_nbr[..., None] == jnp.arange(row_block, dtype=jnp.int32)).astype(jnp.float32)
    rec_range = jnp.arange(n_rec, dtype=jnp.int32)
    lower_tri = (rec_range[None, :] <= rec_range[:, None]).astype(jnp.float32)
    owner_range = jnp.arange(n_owner, dtype=jnp.int32)
    rank_range = jnp.arange(capacity, dtype=jnp.float32)
    mass_cols = cell_mass.reshape(n_cols, layers)
    part_pos = bed_position[0, 0]
    part_vel = bed_velocity[0, 0]
    displace = start_disp
    velocity = start_vel
    for step_id in range(eroded_cells.shape[0]):
        padded = padded_2(displace, (("gx", 1), ("gy", 2)), 1)
        laplace = (
            padded[:, 2:, 1:-1] + padded[:, :-2, 1:-1] + padded[:, 1:-1, 2:] + padded[:, 1:-1, :-2]
        )
        laplace = laplace + depth_sum(displace) - 6.0 * displace
        internal = stiffness[None] * laplace
        forces = internal.reshape(3, n_cols, layers)
        disp_cols = displace.reshape(3, n_cols, layers)
        vel_cols = velocity.reshape(3, n_cols, layers)
        top_layer = disp_cols[:, :, layers - 1]
        seg_rows = jnp.einsum("fc,jc->fj", top_layer, seg_hot, precision=HIGHEST)
        partner = from_partner(seg_rows, "gx", 0)
        facing = jnp.einsum("fi,ji->fj", partner, match_hot, precision=HIGHEST)
        top_add = jnp.einsum(
            "fj,jc->fc", CONTACT_K * (facing - seg_rows), seg_hot, precision=HIGHEST
        )
        forces = forces.at[:, :, layers - 1].add(top_add)
        cells_now = eroded_cells[step_id, 0, 0]
        owners_now = owner_ids[step_id, 0, 0, :, 0]
        col_hot = ((cells_now // layers)[:, None] == col_range[None, :]).astype(jnp.float32)
        layer_hot = ((cells_now % layers)[:, None] == layer_range[None, :]).astype(jnp.float32)
        stacked = jnp.concatenate([mass_cols[None], disp_cols, vel_cols], axis=0)
        picked_cols = jnp.einsum("fcz,ec->fez", stacked, col_hot, precision=HIGHEST)
        picked = jnp.sum(picked_cols * layer_hot[None], axis=2)
        rec_mass = picked[0]
        rec_disp = picked[1:4]
        rec_mom = rec_mass[None] * picked[4:7]
        is_owner = (owners_now[:, None] == owner_range[None, :]).astype(jnp.float32)
        counted = jnp.dot(lower_tri, is_owner, precision=HIGHEST)
        rank_value = jnp.sum(is_owner * counted, axis=1) - 1.0
        rank_hot = (rank_value[:, None] == rank_range[None, :]).astype(jnp.float32)
        pos_blocks = part_pos.reshape(3, n_blocks, row_block)
        drift_blocks = part_vel.reshape(3, n_blocks, row_block)
        bed_near = jnp.einsum("fbs,bkrs->fkbr", pos_blocks, nbr_hot, precision=HIGHEST).reshape(
            3, n_nbr, n_slots
        )
        bed_drift = jnp.einsum("fbs,bkrs->fkbr", drift_blocks, nbr_hot, precision=HIGHEST).reshape(
            3, n_nbr, n_slots
        )
        records = jnp.concatenate([rec_mass[None], rec_disp, rec_mom], axis=0)
        buckets = jnp.einsum("eo,fe,er->ofr", is_owner, records, rank_hot, precision=HIGHEST)
        arrived = lax.all_to_all(buckets, "gy", split_axis=0, concat_axis=0, tiled=True)
        columns = arrived.transpose(1, 2, 0).reshape(7, n_slots)
        slot_mass = columns[0]
        offset = bed_near - columns[1:4][:, None, :]
        weights = 1.0 / (1.0 + jnp.sum(offset * offset, axis=0))
        spring = weights[None] * (PARTICLE_K * slot_mass * offset)
        terms = spring + weights[None] * (
            DRAG_COEF * (slot_mass * bed_drift - columns[4:7][:, None, :])
        )
        slot_force = jnp.sum(terms, axis=1) / n_nbr
        returned = slot_force.reshape(3, capacity, n_owner).transpose(2, 0, 1)
        answers = lax.all_to_all(returned, "gy", split_axis=0, concat_axis=0, tiled=True)
        rec_force = jnp.einsum("ofr,er,eo->fe", answers, rank_hot, is_owner, precision=HIGHEST)
        change = (-TIME_STEP * spring / n_nbr).reshape(3, n_nbr, n_blocks, row_block)
        vel_add = jnp.einsum("fkbr,bkrs->fbs", change, nbr_hot, precision=HIGHEST).reshape(
            3, n_slots
        )
        part_vel = part_vel + vel_add
        part_pos = part_pos + TIME_STEP * part_vel
        rec_add = jnp.einsum("ec,fe,ez->fcz", col_hot, rec_force, layer_hot, precision=HIGHEST)
        forces = (forces + rec_add).reshape(3, cols_x, cols_y, layers)
        velocity = velocity + TIME_STEP * (forces / cell_mass[None])
        displace = displace + TIME_STEP * velocity
    return (displace, velocity)


def solution(mesh):
    return jax.shard_map(
        local,
        mesh=mesh,
        in_specs=(
            P(None, "gx", "gy", None),
            P(None, "gx", "gy", None),
            P("gx", "gy", None),
            P("gx", "gy", None),
            P("gx", "gy", None),
            P("gx", "gy", None),
            P(None, "gx", "gy", None),
            P(None, "gx", "gy", None, None),
            P("gx", "gy", None, None),
            P("gx", "gy", None, None),
            P("gx", "gy", None, None),
        ),
        out_specs=(P(None, "gx", "gy", None), P(None, "gx", "gy", None)),
        check_vma=False,
    )
```

profile of v0, /device:TPU:38, one launch (start us, length us, event | category | flops | bytes accessed | tf_op | source)
XLA Modules:
  0.0 715.9 jit_solution(13677379367658360464)
XLA Ops:
  15.2 8.1 %all-to-all-start = ((f32[16,7,128]{2,1,0:T(8,128)}), f32[16,7,128]{2,1,0:T(8,128)S(1)}, u32[]{:S(2)}, u32[]{:S(2)}) async-start(f32[16,7,128]{2,1,0:T(8,128)} %copy.401), calls=%async_computation | async-start | bytes 131072 | tf_op jit(solution)/shard_map/all_to_all | solution.py:127
  53.1 4.6 collective-permute-start.2
  60.0 6.0 multiply_reduce_fusion.15
  66.5 6.0 fusion.229
  73.3 8.4 %all-to-all-start.1 = ((f32[16,3,128]{2,1,0:T(4,128)}), f32[16,3,128]{2,1,0:T(4,128)S(1)}, u32[]{:S(2)}, u32[]{:S(2)}) async-start(f32[16,3,128]{2,1,0:T(4,128)} %copy.409), calls=%async_computation.1 | async-start | bytes 65536 | tf_op jit(solution)/shard_map/all_to_all | solution.py:138
  81.7 5.5 fusion.251
  126.9 6.5 all-to-all-start.2
  141.3 4.6 collective-permute-start.7
  148.2 6.0 multiply_reduce_fusion.14
  154.7 6.0 fusion.228
  161.5 8.4 %all-to-all-start.3 = ((f32[16,3,128]{2,1,0:T(4,128)}), f32[16,3,128]{2,1,0:T(4,128)S(1)}, u32[]{:S(2)}, u32[]{:S(2)}) async-start(f32[16,3,128]{2,1,0:T(4,128)} %copy.427), calls=%async_computation.3 | async-start | bytes 65536 | tf_op jit(solution)/shard_map/all_to_all | solution.py:138
  169.9 5.5 multiply_add_fusion.20
  215.1 6.5 all-to-all-start.4
  229.2 4.6 collective-permute-start.12
  236.5 6.0 multiply_reduce_fusion.13
  243.1 6.0 fusion.227
  249.9 8.4 %all-to-all-start.5 = ((f32[16,3,128]{2,1,0:T(4,128)}), f32[16,3,128]{2,1,0:T(4,128)S(1)}, u32[]{:S(2)}, u32[]{:S(2)}) async-start(f32[16,3,128]{2,1,0:T(4,128)} %copy.443), calls=%async_computation.5 | async-start | bytes 65536 | tf_op jit(solution)/shard_map/all_to_all | solution.py:138
  258.3 5.4 fusion.249
  303.2 6.4 all-to-all-start.6
  317.2 4.6 collective-permute-start.17
  324.2 6.0 multiply_reduce_fusion.12
  330.7 6.0 fusion.226
  337.6 8.4 %all-to-all-start.7 = ((f32[16,3,128]{2,1,0:T(4,128)}), f32[16,3,128]{2,1,0:T(4,128)S(1)}, u32[]{:S(2)}, u32[]{:S(2)}) async-start(f32[16,3,128]{2,1,0:T(4,128)} %copy.459), calls=%async_computation.7 | async-start | bytes 65536 | tf_op jit(solution)/shard_map/all_to_all | solution.py:138
  346.0 5.4 multiply_add_fusion.18
  390.2 6.4 all-to-all-start.8
  404.2 4.6 collective-permute-start.22
  411.5 6.0 multiply_reduce_fusion.11
  418.0 6.0 fusion.225
  424.8 8.4 %all-to-all-start.9 = ((f32[16,3,128]{2,1,0:T(4,128)}), f32[16,3,128]{2,1,0:T(4,128)S(1)}, u32[]{:S(2)}, u32[]{:S(2)}) async-start(f32[16,3,128]{2,1,0:T(4,128)} %copy.475), calls=%async_computation.9 | async-start | bytes 65536 | tf_op jit(solution)/shard_map/all_to_all | solution.py:138
  433.2 5.4 fusion.247
  476.8 6.4 all-to-all-start.10
  490.8 4.6 collective-permute-start.27
  497.9 6.0 multiply_reduce_fusion.10
  504.4 6.0 fusion.224
  511.2 8.4 %all-to-all-start.11 = ((f32[16,3,128]{2,1,0:T(4,128)}), f32[16,3,128]{2,1,0:T(4,128)S(1)}, u32[]{:S(2)}, u32[]{:S(2)}) async-start(f32[16,3,128]{2,1,0:T(4,128)} %copy.491), calls=%async_computation.11 | async-start | bytes 65536 | tf_op jit(solution)/shard_map/all_to_all | solution.py:138
  519.6 5.4 fusion.246
  563.1 6.4 all-to-all-start.12
  577.1 4.6 collective-permute-start.32
  584.4 6.0 multiply_reduce_fusion.9
  591.0 6.0 fusion.223
  597.8 8.4 %all-to-all-start.13 = ((f32[16,3,128]{2,1,0:T(4,128)}), f32[16,3,128]{2,1,0:T(4,128)S(1)}, u32[]{:S(2)}, u32[]{:S(2)}) async-start(f32[16,3,128]{2,1,0:T(4,128)} %copy.507), calls=%async_computation.13 | async-start | bytes 65536 | tf_op jit(solution)/shard_map/all_to_all | solution.py:138
  606.2 5.4 fusion.245
  648.8 6.4 all-to-all-start.14
  661.9 6.0 multiply_reduce_fusion.8
  668.4 6.0 fusion.222
  675.2 7.0 all-to-all-start.15
  682.3 4.6 collective-permute-start.37
  689.2 5.8 collective-permute-done.38
  (669 shorter events, 416.2 us)
Async XLA Ops:
  15.2 44.4 %all-to-all-start = ((f32[16,7,128]{2,1,0:T(8,128)}), f32[16,7,128]{2,1,0:T(8,128)S(1)}, u32[]{:S(2)}, u32[]{:S(2)}) async-start(f32[16,7,128]{2,1,0:T(8,128)} %copy.401), calls=%async_computation | async-start | bytes 131072 | tf_op jit(solution)/shard_map/all_to_all | solution.py:127
  25.3 24.3 %collective-permute-start.4 = (f32[3,512]{1,0:T(4,128)S(1)}, f32[3,512]{1,0:T(4,128)S(1)}, u32[]{:S(2)}, u32[]{:S(2)}) collective-permute-start(f32[3,512]{1,0:T(4,128)S(1)} %fusion.268), channel_id=1, source_target_pairs={{0,16},{16,0},{32,48},{48,32},{64,80},{80,64},{96,112},{112,96},{1... | collective-permute-start | bytes 18440 | tf_op jit(solution)/shard_map/ppermute | solution.py:33
  25.3 26.3 %collective-permute-start.1 = (f32[3,1,32,128]{3,2,1,0:T(8,128)S(1)}, f32[3,1,32,128]{3,2,1,0:T(8,128)S(1)}, u32[]{:S(2)}, u32[]{:S(2)}) collective-permute-start(f32[3,1,32,128]{3,2,1,0:T(8,128)S(1)} %get-tuple-element.161), channel_id=1, source_target_pairs={{0,16},{16,32},{32,48},{48,64},{64,80},{80,96},{96,112},{1,17},{17... | collective-permute-start | bytes 147464 | tf_op jit(solution)/shard_map/ppermute | solution.py:21
  27.7 24.1 %collective-permute-start = (f32[3,1,32,128]{3,2,1,0:T(8,128)S(1)}, f32[3,1,32,128]{3,2,1,0:T(8,128)S(1)}, u32[]{:S(2)}, u32[]{:S(2)}) collective-permute-start(f32[3,1,32,128]{3,2,1,0:T(8,128)S(1)} %get-tuple-element.160), channel_id=1, source_target_pairs={{16,0},{32,16},{48,32},{64,48},{80,64},{96,80},{112,96},{17,1},{33... | collective-permute-start | bytes 147464 | tf_op jit(solution)/shard_map/ppermute | solution.py:23
  53.1 35.8 %collective-permute-start.2 = (f32[3,34,1,128]{3,2,1,0:T(1,128)S(1)}, f32[3,34,1,128]{3,2,1,0:T(1,128)S(1)}, u32[]{:S(2)}, u32[]{:S(2)}) collective-permute-start(f32[3,34,1,128]{3,2,1,0:T(1,128)S(1)} %get-tuple-element.128), channel_id=1, source_target_pairs={{1,0},{2,1},{3,2},{4,3},{5,4},{6,5},{7,6},{8,7},{9,8},{10,9},{11,1... | collective-permute-start | bytes 156680 | tf_op jit(solution)/shard_map/ppermute | solution.py:23
  57.7 31.2 %collective-permute-start.3 = (f32[3,34,1,128]{3,2,1,0:T(1,128)S(1)}, f32[3,34,1,128]{3,2,1,0:T(1,128)S(1)}, u32[]{:S(2)}, u32[]{:S(2)}) collective-permute-start(f32[3,34,1,128]{3,2,1,0:T(1,128)S(1)} %get-tuple-element.129), channel_id=1, source_target_pairs={{0,1},{1,2},{2,3},{3,4},{4,5},{5,6},{6,7},{7,8},{8,9},{9,10},{10,1... | collective-permute-start | bytes 156680 | tf_op jit(solution)/shard_map/ppermute | solution.py:21
  73.3 14.6 %all-to-all-start.1 = ((f32[16,3,128]{2,1,0:T(4,128)}), f32[16,3,128]{2,1,0:T(4,128)S(1)}, u32[]{:S(2)}, u32[]{:S(2)}) async-start(f32[16,3,128]{2,1,0:T(4,128)} %copy.409), calls=%async_computation.1 | async-start | bytes 65536 | tf_op jit(solution)/shard_map/all_to_all | solution.py:138
  125.7 12.2 %collective-permute-start.9 = (f32[3,512]{1,0:T(4,128)S(1)}, f32[3,512]{1,0:T(4,128)S(1)}, u32[]{:S(2)}, u32[]{:S(2)}) collective-permute-start(f32[3,512]{1,0:T(4,128)S(1)} %fusion.83), channel_id=1, source_target_pairs={{0,16},{16,0},{32,48},{48,32},{64,80},{80,64},{96,112},{112,96},{1... | collective-permute-start | bytes 18440 | tf_op jit(solution)/shard_map/ppermute | solution.py:33
  126.9 20.9 %all-to-all-start.2 = ((f32[16,7,128]{2,1,0:T(8,128)}), f32[16,7,128]{2,1,0:T(8,128)S(1)}, u32[]{:S(2)}, u32[]{:S(2)}) async-start(f32[16,7,128]{2,1,0:T(8,128)} %copy.420), calls=%async_computation.2 | async-start | bytes 131072 | tf_op jit(solution)/shard_map/all_to_all | solution.py:127
  133.4 6.6 collective-permute-start.5
  141.3 35.8 %collective-permute-start.7 = (f32[3,34,1,128]{3,2,1,0:T(1,128)S(1)}, f32[3,34,1,128]{3,2,1,0:T(1,128)S(1)}, u32[]{:S(2)}, u32[]{:S(2)}) collective-permute-start(f32[3,34,1,128]{3,2,1,0:T(1,128)S(1)} %get-tuple-element.126), channel_id=1, source_target_pairs={{1,0},{2,1},{3,2},{4,3},{5,4},{6,5},{7,6},{8,7},{9,8},{10,9},{11,1... | collective-permute-start | bytes 156680 | tf_op jit(solution)/shard_map/ppermute | solution.py:23
  145.9 31.3 %collective-permute-start.8 = (f32[3,34,1,128]{3,2,1,0:T(1,128)S(1)}, f32[3,34,1,128]{3,2,1,0:T(1,128)S(1)}, u32[]{:S(2)}, u32[]{:S(2)}) collective-permute-start(f32[3,34,1,128]{3,2,1,0:T(1,128)S(1)} %get-tuple-element.127), channel_id=1, source_target_pairs={{0,1},{1,2},{2,3},{3,4},{4,5},{5,6},{6,7},{7,8},{8,9},{9,10},{10,1... | collective-permute-start | bytes 156680 | tf_op jit(solution)/shard_map/ppermute | solution.py:21
  161.5 14.6 %all-to-all-start.3 = ((f32[16,3,128]{2,1,0:T(4,128)}), f32[16,3,128]{2,1,0:T(4,128)S(1)}, u32[]{:S(2)}, u32[]{:S(2)}) async-start(f32[16,3,128]{2,1,0:T(4,128)} %copy.427), calls=%async_computation.3 | async-start | bytes 65536 | tf_op jit(solution)/shard_map/all_to_all | solution.py:138
  214.0 12.0 %collective-permute-start.14 = (f32[3,512]{1,0:T(4,128)S(1)}, f32[3,512]{1,0:T(4,128)S(1)}, u32[]{:S(2)}, u32[]{:S(2)}) collective-permute-start(f32[3,512]{1,0:T(4,128)S(1)} %fusion.81), channel_id=1, source_target_pairs={{0,16},{16,0},{32,48},{48,32},{64,80},{80,64},{96,112},{112,96},{1... | collective-permute-start | bytes 18440 | tf_op jit(solution)/shard_map/ppermute | solution.py:33
  215.1 21.1 %all-to-all-start.4 = ((f32[16,7,128]{2,1,0:T(8,128)}), f32[16,7,128]{2,1,0:T(8,128)S(1)}, u32[]{:S(2)}, u32[]{:S(2)}) async-start(f32[16,7,128]{2,1,0:T(8,128)} %copy.436), calls=%async_computation.4 | async-start | bytes 131072 | tf_op jit(solution)/shard_map/all_to_all | solution.py:127
  221.5 6.6 collective-permute-start.10
  229.2 36.3 %collective-permute-start.12 = (f32[3,34,1,128]{3,2,1,0:T(1,128)S(1)}, f32[3,34,1,128]{3,2,1,0:T(1,128)S(1)}, u32[]{:S(2)}, u32[]{:S(2)}) collective-permute-start(f32[3,34,1,128]{3,2,1,0:T(1,128)S(1)} %get-tuple-element.124), channel_id=1, source_target_pairs={{1,0},{2,1},{3,2},{4,3},{5,4},{6,5},{7,6},{8,7},{9,8},{10,9},{11,1... | collective-permute-start | bytes 156680 | tf_op jit(solution)/shard_map/ppermute | solution.py:23
  233.8 31.7 %collective-permute-start.13 = (f32[3,34,1,128]{3,2,1,0:T(1,128)S(1)}, f32[3,34,1,128]{3,2,1,0:T(1,128)S(1)}, u32[]{:S(2)}, u32[]{:S(2)}) collective-permute-start(f32[3,34,1,128]{3,2,1,0:T(1,128)S(1)} %get-tuple-element.125), channel_id=1, source_target_pairs={{0,1},{1,2},{2,3},{3,4},{4,5},{5,6},{6,7},{7,8},{8,9},{9,10},{10,1... | collective-permute-start | bytes 156680 | tf_op jit(solution)/shard_map/ppermute | solution.py:21
  249.9 14.6 %all-to-all-start.5 = ((f32[16,3,128]{2,1,0:T(4,128)}), f32[16,3,128]{2,1,0:T(4,128)S(1)}, u32[]{:S(2)}, u32[]{:S(2)}) async-start(f32[16,3,128]{2,1,0:T(4,128)} %copy.443), calls=%async_computation.5 | async-start | bytes 65536 | tf_op jit(solution)/shard_map/all_to_all | solution.py:138
  302.1 11.9 %collective-permute-start.19 = (f32[3,512]{1,0:T(4,128)S(1)}, f32[3,512]{1,0:T(4,128)S(1)}, u32[]{:S(2)}, u32[]{:S(2)}) collective-permute-start(f32[3,512]{1,0:T(4,128)S(1)} %fusion.79), channel_id=1, source_target_pairs={{0,16},{16,0},{32,48},{48,32},{64,80},{80,64},{96,112},{112,96},{1... | collective-permute-start | bytes 18440 | tf_op jit(solution)/shard_map/ppermute | solution.py:33
  303.2 20.7 %all-to-all-start.6 = ((f32[16,7,128]{2,1,0:T(8,128)}), f32[16,7,128]{2,1,0:T(8,128)S(1)}, u32[]{:S(2)}, u32[]{:S(2)}) async-start(f32[16,7,128]{2,1,0:T(8,128)} %copy.452), calls=%async_computation.6 | async-start | bytes 131072 | tf_op jit(solution)/shard_map/all_to_all | solution.py:127
  309.6 6.6 collective-permute-start.15
  317.2 36.0 %collective-permute-start.17 = (f32[3,34,1,128]{3,2,1,0:T(1,128)S(1)}, f32[3,34,1,128]{3,2,1,0:T(1,128)S(1)}, u32[]{:S(2)}, u32[]{:S(2)}) collective-permute-start(f32[3,34,1,128]{3,2,1,0:T(1,128)S(1)} %get-tuple-element.122), channel_id=1, source_target_pairs={{1,0},{2,1},{3,2},{4,3},{5,4},{6,5},{7,6},{8,7},{9,8},{10,9},{11,1... | collective-permute-start | bytes 156680 | tf_op jit(solution)/shard_map/ppermute | solution.py:23
  321.7 31.4 %collective-permute-start.18 = (f32[3,34,1,128]{3,2,1,0:T(1,128)S(1)}, f32[3,34,1,128]{3,2,1,0:T(1,128)S(1)}, u32[]{:S(2)}, u32[]{:S(2)}) collective-permute-start(f32[3,34,1,128]{3,2,1,0:T(1,128)S(1)} %get-tuple-element.123), channel_id=1, source_target_pairs={{0,1},{1,2},{2,3},{3,4},{4,5},{5,6},{6,7},{7,8},{8,9},{9,10},{10,1... | collective-permute-start | bytes 156680 | tf_op jit(solution)/shard_map/ppermute | solution.py:21
  337.6 14.6 %all-to-all-start.7 = ((f32[16,3,128]{2,1,0:T(4,128)}), f32[16,3,128]{2,1,0:T(4,128)S(1)}, u32[]{:S(2)}, u32[]{:S(2)}) async-start(f32[16,3,128]{2,1,0:T(4,128)} %copy.459), calls=%async_computation.7 | async-start | bytes 65536 | tf_op jit(solution)/shard_map/all_to_all | solution.py:138
  389.2 12.0 %collective-permute-start.24 = (f32[3,512]{1,0:T(4,128)S(1)}, f32[3,512]{1,0:T(4,128)S(1)}, u32[]{:S(2)}, u32[]{:S(2)}) collective-permute-start(f32[3,512]{1,0:T(4,128)S(1)} %fusion.77), channel_id=1, source_target_pairs={{0,16},{16,0},{32,48},{48,32},{64,80},{80,64},{96,112},{112,96},{1... | collective-permute-start | bytes 18440 | tf_op jit(solution)/shard_map/ppermute | solution.py:33
  390.2 20.9 %all-to-all-start.8 = ((f32[16,7,128]{2,1,0:T(8,128)}), f32[16,7,128]{2,1,0:T(8,128)S(1)}, u32[]{:S(2)}, u32[]{:S(2)}) async-start(f32[16,7,128]{2,1,0:T(8,128)} %copy.468), calls=%async_computation.8 | async-start | bytes 131072 | tf_op jit(solution)/shard_map/all_to_all | solution.py:127
  404.2 35.6 %collective-permute-start.22 = (f32[3,34,1,128]{3,2,1,0:T(1,128)S(1)}, f32[3,34,1,128]{3,2,1,0:T(1,128)S(1)}, u32[]{:S(2)}, u32[]{:S(2)}) collective-permute-start(f32[3,34,1,128]{3,2,1,0:T(1,128)S(1)} %get-tuple-element.120), channel_id=1, source_target_pairs={{1,0},{2,1},{3,2},{4,3},{5,4},{6,5},{7,6},{8,7},{9,8},{10,9},{11,1... | collective-permute-start | bytes 156680 | tf_op jit(solution)/shard_map/ppermute | solution.py:23
  408.8 31.1 %collective-permute-start.23 = (f32[3,34,1,128]{3,2,1,0:T(1,128)S(1)}, f32[3,34,1,128]{3,2,1,0:T(1,128)S(1)}, u32[]{:S(2)}, u32[]{:S(2)}) collective-permute-start(f32[3,34,1,128]{3,2,1,0:T(1,128)S(1)} %get-tuple-element.121), channel_id=1, source_target_pairs={{0,1},{1,2},{2,3},{3,4},{4,5},{5,6},{6,7},{7,8},{8,9},{9,10},{10,1... | collective-permute-start | bytes 156680 | tf_op jit(solution)/shard_map/ppermute | solution.py:21
  424.8 14.6 %all-to-all-start.9 = ((f32[16,3,128]{2,1,0:T(4,128)}), f32[16,3,128]{2,1,0:T(4,128)S(1)}, u32[]{:S(2)}, u32[]{:S(2)}) async-start(f32[16,3,128]{2,1,0:T(4,128)} %copy.475), calls=%async_computation.9 | async-start | bytes 65536 | tf_op jit(solution)/shard_map/all_to_all | solution.py:138
  475.8 11.9 %collective-permute-start.29 = (f32[3,512]{1,0:T(4,128)S(1)}, f32[3,512]{1,0:T(4,128)S(1)}, u32[]{:S(2)}, u32[]{:S(2)}) collective-permute-start(f32[3,512]{1,0:T(4,128)S(1)} %fusion.75), channel_id=1, source_target_pairs={{0,16},{16,0},{32,48},{48,32},{64,80},{80,64},{96,112},{112,96},{1... | collective-permute-start | bytes 18440 | tf_op jit(solution)/shard_map/ppermute | solution.py:33
  476.8 20.7 %all-to-all-start.10 = ((f32[16,7,128]{2,1,0:T(8,128)}), f32[16,7,128]{2,1,0:T(8,128)S(1)}, u32[]{:S(2)}, u32[]{:S(2)}) async-start(f32[16,7,128]{2,1,0:T(8,128)} %copy.484), calls=%async_computation.10 | async-start | bytes 131072 | tf_op jit(solution)/shard_map/all_to_all | solution.py:127
  490.8 35.4 %collective-permute-start.27 = (f32[3,34,1,128]{3,2,1,0:T(1,128)S(1)}, f32[3,34,1,128]{3,2,1,0:T(1,128)S(1)}, u32[]{:S(2)}, u32[]{:S(2)}) collective-permute-start(f32[3,34,1,128]{3,2,1,0:T(1,128)S(1)} %get-tuple-element.118), channel_id=1, source_target_pairs={{1,0},{2,1},{3,2},{4,3},{5,4},{6,5},{7,6},{8,7},{9,8},{10,9},{11,1... | collective-permute-start | bytes 156680 | tf_op jit(solution)/shard_map/ppermute | solution.py:23
  495.4 30.8 %collective-permute-start.28 = (f32[3,34,1,128]{3,2,1,0:T(1,128)S(1)}, f32[3,34,1,128]{3,2,1,0:T(1,128)S(1)}, u32[]{:S(2)}, u32[]{:S(2)}) collective-permute-start(f32[3,34,1,128]{3,2,1,0:T(1,128)S(1)} %get-tuple-element.119), channel_id=1, source_target_pairs={{0,1},{1,2},{2,3},{3,4},{4,5},{5,6},{6,7},{7,8},{8,9},{9,10},{10,1... | collective-permute-start | bytes 156680 | tf_op jit(solution)/shard_map/ppermute | solution.py:21
  511.2 14.6 %all-to-all-start.11 = ((f32[16,3,128]{2,1,0:T(4,128)}), f32[16,3,128]{2,1,0:T(4,128)S(1)}, u32[]{:S(2)}, u32[]{:S(2)}) async-start(f32[16,3,128]{2,1,0:T(4,128)} %copy.491), calls=%async_computation.11 | async-start | bytes 65536 | tf_op jit(solution)/shard_map/all_to_all | solution.py:138
  562.1 12.0 %collective-permute-start.34 = (f32[3,512]{1,0:T(4,128)S(1)}, f32[3,512]{1,0:T(4,128)S(1)}, u32[]{:S(2)}, u32[]{:S(2)}) collective-permute-start(f32[3,512]{1,0:T(4,128)S(1)} %fusion.73), channel_id=1, source_target_pairs={{0,16},{16,0},{32,48},{48,32},{64,80},{80,64},{96,112},{112,96},{1... | collective-permute-start | bytes 18440 | tf_op jit(solution)/shard_map/ppermute | solution.py:33
  563.1 20.9 %all-to-all-start.12 = ((f32[16,7,128]{2,1,0:T(8,128)}), f32[16,7,128]{2,1,0:T(8,128)S(1)}, u32[]{:S(2)}, u32[]{:S(2)}) async-start(f32[16,7,128]{2,1,0:T(8,128)} %copy.500), calls=%async_computation.12 | async-start | bytes 131072 | tf_op jit(solution)/shard_map/all_to_all | solution.py:127
  569.6 6.0 collective-permute-start.30
  577.1 35.6 %collective-permute-start.32 = (f32[3,34,1,128]{3,2,1,0:T(1,128)S(1)}, f32[3,34,1,128]{3,2,1,0:T(1,128)S(1)}, u32[]{:S(2)}, u32[]{:S(2)}) collective-permute-start(f32[3,34,1,128]{3,2,1,0:T(1,128)S(1)} %get-tuple-element.116), channel_id=1, source_target_pairs={{1,0},{2,1},{3,2},{4,3},{5,4},{6,5},{7,6},{8,7},{9,8},{10,9},{11,1... | collective-permute-start | bytes 156680 | tf_op jit(solution)/shard_map/ppermute | solution.py:23
  581.7 31.1 %collective-permute-start.33 = (f32[3,34,1,128]{3,2,1,0:T(1,128)S(1)}, f32[3,34,1,128]{3,2,1,0:T(1,128)S(1)}, u32[]{:S(2)}, u32[]{:S(2)}) collective-permute-start(f32[3,34,1,128]{3,2,1,0:T(1,128)S(1)} %get-tuple-element.117), channel_id=1, source_target_pairs={{0,1},{1,2},{2,3},{3,4},{4,5},{5,6},{6,7},{7,8},{8,9},{9,10},{10,1... | collective-permute-start | bytes 156680 | tf_op jit(solution)/shard_map/ppermute | solution.py:21
  597.8 14.6 %all-to-all-start.13 = ((f32[16,3,128]{2,1,0:T(4,128)}), f32[16,3,128]{2,1,0:T(4,128)S(1)}, u32[]{:S(2)}, u32[]{:S(2)}) async-start(f32[16,3,128]{2,1,0:T(4,128)} %copy.507), calls=%async_computation.13 | async-start | bytes 65536 | tf_op jit(solution)/shard_map/all_to_all | solution.py:138
  647.8 12.0 %collective-permute-start.39 = (f32[3,512]{1,0:T(4,128)S(1)}, f32[3,512]{1,0:T(4,128)S(1)}, u32[]{:S(2)}, u32[]{:S(2)}) collective-permute-start(f32[3,512]{1,0:T(4,128)S(1)} %fusion.71), channel_id=1, source_target_pairs={{0,16},{16,0},{32,48},{48,32},{64,80},{80,64},{96,112},{112,96},{1... | collective-permute-start | bytes 18440 | tf_op jit(solution)/shard_map/ppermute | solution.py:33
  648.8 12.7 %all-to-all-start.14 = ((f32[16,7,128]{2,1,0:T(8,128)}), f32[16,7,128]{2,1,0:T(8,128)S(1)}, u32[]{:S(2)}, u32[]{:S(2)}) async-start(f32[16,7,128]{2,1,0:T(8,128)} %copy.516), calls=%async_computation.14 | async-start | bytes 131072 | tf_op jit(solution)/shard_map/all_to_all | solution.py:127
  655.3 26.9 %collective-permute-start.35 = (f32[3,1,32,128]{3,2,1,0:T(8,128)S(1)}, f32[3,1,32,128]{3,2,1,0:T(8,128)S(1)}, u32[]{:S(2)}, u32[]{:S(2)}) collective-permute-start(f32[3,1,32,128]{3,2,1,0:T(8,128)S(1)} %get-tuple-element.133), channel_id=1, source_target_pairs={{16,0},{32,16},{48,32},{64,48},{80,64},{96,80},{112,96},{17,1},{33... | collective-permute-start | bytes 147464 | tf_op jit(solution)/shard_map/ppermute | solution.py:23
  657.2 25.0 %collective-permute-start.36 = (f32[3,1,32,128]{3,2,1,0:T(8,128)S(1)}, f32[3,1,32,128]{3,2,1,0:T(8,128)S(1)}, u32[]{:S(2)}, u32[]{:S(2)}) collective-permute-start(f32[3,1,32,128]{3,2,1,0:T(8,128)S(1)} %get-tuple-element.132), channel_id=1, source_target_pairs={{0,16},{16,32},{32,48},{48,64},{64,80},{80,96},{96,112},{1,17},{17... | collective-permute-start | bytes 147464 | tf_op jit(solution)/shard_map/ppermute | solution.py:21
  675.2 13.6 %all-to-all-start.15 = ((f32[16,3,128]{2,1,0:T(4,128)}), f32[16,3,128]{2,1,0:T(4,128)S(1)}, u32[]{:S(2)}, u32[]{:S(2)}) async-start(f32[16,3,128]{2,1,0:T(4,128)} %copy.523), calls=%async_computation.15 | async-start | bytes 65536 | tf_op jit(solution)/shard_map/all_to_all | solution.py:138
  682.3 6.9 collective-permute-start.37
  686.9 8.1 %collective-permute-start.38 = (f32[3,34,1,128]{3,2,1,0:T(1,128)S(1)}, f32[3,34,1,128]{3,2,1,0:T(1,128)S(1)}, u32[]{:S(2)}, u32[]{:S(2)}) collective-permute-start(f32[3,34,1,128]{3,2,1,0:T(1,128)S(1)} %get-tuple-element.115), channel_id=1, source_target_pairs={{0,1},{1,2},{2,3},{3,4},{4,5},{5,6},{6,7},{7,8},{8,9},{9,10},{10,1... | collective-permute-start | bytes 156680 | tf_op jit(solution)/shard_map/ppermute | solution.py:21
  (104 other events, 688.4 us)
where the time goes:
time: 728 us; the launch traced here: 716 us
  matrix products  221 us (30%)
  starting transfers between devices  209 us (29%)
  local copies, waits for them, and re-layouts  164 us (23%)
  other arithmetic  97.8 us (13%)
  waiting for transfers between devices  19.4 us (3%)
    all_to_all x8, starting transfers between devices, local(): lax.all_to_all(returned, 'gy', split_axis=0, concat_axis=0, tiled=True)  65.6 us
    ppermute x16, starting transfers between devices, padded_2(): lax.ppermute(head, axis, [((i + 1) % count, i) for i in range(ends)])  53.6 us
    all_to_all x8, starting transfers between devices, local(): lax.all_to_all(buckets, 'gy', split_axis=0, concat_axis=0, tiled=True)  53.2 us
    dot_general x8, matrix products, local(): jnp.einsum('fbs,bkrs->fkbr', pos_blocks, nbr_hot, precision=HIGHEST)  48.2 us
    dot_general x8, matrix products, local(): jnp.einsum('fbs,bkrs->fkbr', drift_blocks, nbr_hot, precision=HIGHEST)  47.9 us
    dot_general x7, matrix products, local(): jnp.einsum('fkbr,bkrs->fbs', change, nbr_hot, precision=HIGHEST)  38.1 us
    ppermute x16, starting transfers between devices, padded_2(): lax.ppermute(tail, axis, [(i, (i + 1) % count) for i in range(ends)])  36.8 us
    add x8, other arithmetic, local(): displace = displace + TIME_STEP * velocity  31.2 us
  transfers between devices with their start and end apart: 56, of which 15 were waited for; matrix products, arithmetic and copies ran while one was open for 27% of the time, Pallas kernels for 0%

commit v1 on v0

v1 whole, which is shorter than its diff:
```python
import jax
import jax.numpy as jnp
from jax import lax
from jax.sharding import PartitionSpec as P

TIME_STEP = 0.2
CONTACT_K = 0.5
PARTICLE_K = 1.0
DRAG_COEF = 0.5
HIGHEST = lax.Precision.HIGHEST


def shift_pairs(axis, up):
    count = lax.axis_size(axis)
    if up:
        return [(i, i + 1) for i in range(count - 1)]
    return [(i + 1, i) for i in range(count - 1)]


def from_partner(value, axis, stride):
    mask = 2**stride
    pairs = [(source, source ^ mask) for source in range(lax.axis_size(axis))]
    return lax.ppermute(value, axis, pairs)


def split3(x):
    hi = lax.reduce_precision(x, exponent_bits=8, mantissa_bits=7)
    rest = x - hi
    mid = lax.reduce_precision(rest, exponent_bits=8, mantissa_bits=7)
    lo = rest - mid
    return jnp.stack([hi, mid, lo]).astype(jnp.bfloat16)


def laplacian(d):
    xm_face = lax.ppermute(d[:, -1], "gx", shift_pairs("gx", True))
    xp_face = lax.ppermute(d[:, 0], "gx", shift_pairs("gx", False))
    ym_face = lax.ppermute(d[:, :, -1], "gy", shift_pairs("gy", True))
    yp_face = lax.ppermute(d[:, :, 0], "gy", shift_pairs("gy", False))
    xp = jnp.concatenate([d[:, 1:], xp_face[:, None]], axis=1)
    xm = jnp.concatenate([xm_face[:, None], d[:, :-1]], axis=1)
    yp = jnp.concatenate([d[:, :, 1:], yp_face[:, :, None]], axis=2)
    ym = jnp.concatenate([ym_face[:, :, None], d[:, :, :-1]], axis=2)
    zeros = jnp.zeros_like(d[..., :1])
    zp = jnp.concatenate([d[..., 1:], zeros], axis=-1)
    zm = jnp.concatenate([zeros, d[..., :-1]], axis=-1)
    lap = xp + xm + yp + ym
    return lap + (zp + zm) - 6.0 * d


def local(
    start_disp,
    start_vel,
    stiffness,
    cell_mass,
    contact_cells,
    contact_match,
    eroded_cells,
    owner_ids,
    bed_position,
    bed_velocity,
    bed_neighbours,
):
    cols_x = start_disp.shape[1]
    cols_y = start_disp.shape[2]
    layers = start_disp.shape[3]
    n_cols = cols_x * cols_y
    n_owner = lax.axis_size("gy")
    n_slots = bed_position.shape[3]
    capacity = n_slots // n_owner
    row_block = min(128, n_slots)
    n_blocks = n_slots // row_block
    n_nbr = bed_neighbours.shape[2]
    n_seg = contact_cells.shape[2]
    n_steps = eroded_cells.shape[0]
    lane = jnp.arange(layers, dtype=jnp.int32)

    cc = contact_cells[0, 0]
    match_hot = (
        contact_match[0, 0][:, None] == jnp.arange(n_seg, dtype=jnp.int32)[None, :]
    ).astype(jnp.float32)

    cells_all = eroded_cells[:, 0, 0]
    owners_all = owner_ids[:, 0, 0, :, 0]
    is_owner = owners_all[..., None] == jnp.arange(n_owner, dtype=jnp.int32)
    counted = jnp.cumsum(is_owner.astype(jnp.int32), axis=1)
    rank_all = jnp.sum(jnp.where(is_owner, counted, 0), axis=-1) - 1
    slot_all = owners_all * capacity + rank_all
    col_all = cells_all // layers
    z_all = cells_all % layers
    mass_cols = cell_mass.reshape(n_cols, layers)
    mass_all = jnp.sum(
        jnp.take(mass_cols, col_all, axis=0) * (z_all[..., None] == lane), axis=-1
    )
    upd_cols = jnp.concatenate([jnp.broadcast_to(cc, (n_steps, n_seg)), col_all], axis=1)
    flat_all = upd_cols[:, None, :] + n_cols * jnp.arange(3, dtype=jnp.int32)[None, :, None]
    upd_lane = jnp.concatenate(
        [jnp.full((n_steps, n_seg), layers - 1, jnp.int32), z_all], axis=1
    )

    local_nbr = bed_neighbours[0, 0].reshape(n_nbr, n_blocks, row_block).transpose(1, 0, 2)
    nbr_hot = (
        local_nbr.reshape(n_blocks, n_nbr * row_block)[..., None]
        == jnp.arange(row_block, dtype=jnp.int32)
    ).astype(jnp.bfloat16)

    part_pos = bed_position[0, 0]
    part_vel = bed_velocity[0, 0]
    displace = start_disp
    velocity = start_vel
    for step_id in range(n_steps):
        laplace = laplacian(displace)
        internal = stiffness[None] * laplace

        disp_flat = displace.reshape(3 * n_cols, layers)
        vel_flat = velocity.reshape(3 * n_cols, layers)
        flat_rows = flat_all[step_id]
        lane_hot = upd_lane[step_id][:, None] == lane
        picked = jnp.take(disp_flat, flat_rows.reshape(-1), axis=0).reshape(3, -1, layers)
        picked = jnp.sum(jnp.where(lane_hot[None], picked, 0.0), axis=-1)
        seg_rows = picked[:, :n_seg]
        rec_disp = picked[:, n_seg:]
        rec_rows = flat_rows[:, n_seg:].reshape(-1)
        rec_velo = jnp.take(vel_flat, rec_rows, axis=0).reshape(3, -1, layers)
        rec_velo = jnp.sum(jnp.where(lane_hot[None, n_seg:], rec_velo, 0.0), axis=-1)

        partner = from_partner(seg_rows, "gx", 0)
        facing = jnp.einsum("fi,ji->fj", partner, match_hot, precision=HIGHEST)
        pull = CONTACT_K * (facing - seg_rows)

        rec_mass = mass_all[step_id]
        rec_mom = rec_mass[None] * rec_velo
        records = jnp.concatenate(
            [rec_mass[None], rec_disp, rec_mom, jnp.zeros_like(rec_mass)[None]], axis=0
        )
        slot = slot_all[step_id]
        buckets = jnp.zeros((n_slots, 8), jnp.float32).at[slot].set(records.T)
        buckets = buckets.reshape(n_owner, capacity, 8)
        arrived = lax.all_to_all(buckets, "gy", split_axis=0, concat_axis=0, tiled=True)
        columns = arrived.transpose(2, 1, 0).reshape(8, n_slots)
        slot_mass = columns[0]

        state = jnp.concatenate([part_pos, part_vel], axis=0).reshape(6, n_blocks, row_block)
        state_split = split3(state).reshape(3 * 6, n_blocks, row_block)
        gathered = jnp.einsum(
            "pbs,bqs->pbq", state_split, nbr_hot, preferred_element_type=jnp.float32
        ).reshape(3, 6, n_blocks, n_nbr, row_block)
        gathered = gathered[0] + gathered[1] + gathered[2]
        gathered = gathered.transpose(0, 2, 1, 3).reshape(6, n_nbr, n_slots)
        bed_near = gathered[0:3]
        bed_drift = gathered[3:6]

        offset = bed_near - columns[1:4][:, None, :]
        weights = 1.0 / (1.0 + jnp.sum(offset * offset, axis=0))
        spring = weights[None] * (PARTICLE_K * slot_mass * offset)
        terms = spring + weights[None] * (
            DRAG_COEF * (slot_mass * bed_drift - columns[4:7][:, None, :])
        )
        slot_force = jnp.sum(terms, axis=1) / n_nbr
        returned = slot_force.reshape(3, capacity, n_owner).transpose(2, 1, 0)
        answers = lax.all_to_all(returned, "gy", split_axis=0, concat_axis=0, tiled=True)
        rec_force = answers.reshape(n_slots, 3)[slot].T

        change = (-TIME_STEP * spring / n_nbr).reshape(3, n_nbr, n_blocks, row_block)
        change = change.transpose(0, 2, 1, 3).reshape(3, n_blocks, n_nbr * row_block)
        change_split = split3(change).reshape(9, n_blocks, n_nbr * row_block)
        vel_add = jnp.einsum(
            "pbq,bqs->pbs", change_split, nbr_hot, preferred_element_type=jnp.float32
        ).reshape(3, 3, n_slots)
        vel_add = vel_add[0] + vel_add[1] + vel_add[2]
        part_vel = part_vel + vel_add
        part_pos = part_pos + TIME_STEP * part_vel

        values = jnp.concatenate([pull, rec_force], axis=1)
        rows = jnp.where(lane_hot[None], values[:, :, None], 0.0)
        extra = jnp.zeros((3 * n_cols, layers), jnp.float32).at[flat_rows.reshape(-1)].add(
            rows.reshape(-1, layers)
        )
        forces = internal + extra.reshape(3, cols_x, cols_y, layers)
        velocity = velocity + TIME_STEP * (forces / cell_mass[None])
        displace = displace + TIME_STEP * velocity
    return (displace, velocity)


def solution(mesh):
    return jax.shard_map(
        local,
        mesh=mesh,
        in_specs=(
            P(None, "gx", "gy", None),
            P(None, "gx", "gy", None),
            P("gx", "gy", None),
            P("gx", "gy", None),
            P("gx", "gy", None),
            P("gx", "gy", None),
            P(None, "gx", "gy", None),
            P(None, "gx", "gy", None, None),
            P("gx", "gy", None, None),
            P("gx", "gy", None, None),
            P("gx", "gy", None, None),
        ),
        out_specs=(P(None, "gx", "gy", None), P(None, "gx", "gy", None)),
        check_vma=False,
    )
```

time: 728 us -> 923 us (1.27)
  other arithmetic: 97.8 us -> 298 us
  matrix products: 221 us -> 92 us
  local copies, waits for them, and re-layouts: 164 us -> 287 us
  waiting for transfers between devices: 19.4 us -> 5.62 us
  starting transfers between devices: 209 us -> 219 us
    scatter-add x0 -> x8, other arithmetic: none -> 147 us  [local(): jnp.zeros((3 * n_cols, layers), jnp.float32).at[flat_rows.reshape(-1)]]
    gather x0 -> x33, local copies, waits for them, and re-layouts: none -> 147 us  [the longest x8 92.6 us: local(): jnp.take(disp_flat, flat_rows.reshape(-1), axis=0).reshape(3, -1, layers)]
    dot_general x71 -> x15, matrix products: 190 us -> 80.4 us  [the longest x8 42.5 us: local(): jnp.einsum('pbs,bqs->pbq', state_split, nbr_hot, preferred_element_type=j...]
    reshape x24 -> x23, local copies, waits for them, and re-layouts: 52.7 us -> 11.4 us  [the longest x8 11.1 us: local(): buckets = buckets.reshape(n_owner, capacity, 8)]
    slice x43 -> x63, local copies, waits for them, and re-layouts: 26.3 us -> 67.5 us  [the longest x8 18.2 us: laplacian(): zp = jnp.concatenate([d[..., 1:], zeros], axis=-1)]
    reduce_sum x8 -> x27, other arithmetic: 2.12 us -> 32.2 us  [the longest x8 19.3 us: local(): picked = jnp.sum(jnp.where(lane_hot[None], picked, 0.0), axis=-1)]
    mul x16 -> x8, other arithmetic: 29.5 us -> 3.35 us  [the longest x7 3.35 us: local(): rec_mom = rec_mass[None] * rec_velo]
    unnamed x8 -> x0, matrix products: 25.8 us -> none
  transfers between devices with their start and end apart: 56 -> 56, of which waited for: 15 -> 1; matrix products, arithmetic and copies ran while one was open for 27% -> 44% of each run, Pallas kernels for 0% -> 0%
where the time goes in v1:
time: 923 us; the launch traced here: 908 us
  other arithmetic  298 us (32%)
  local copies, waits for them, and re-layouts  287 us (31%)
  starting transfers between devices  219 us (24%)
  matrix products  92 us (10%)
    scatter-add x8, other arithmetic, local(): jnp.zeros((3 * n_cols, layers), jnp.float32).at[flat_rows.reshape(-1)]  147 us
    gather x8, local copies, waits for them, and re-layouts, local(): jnp.take(disp_flat, flat_rows.reshape(-1), axis=0).reshape(3, -1, layers)  92.6 us
    all_to_all x8, starting transfers between devices, local(): lax.all_to_all(returned, 'gy', split_axis=0, concat_axis=0, tiled=True)  69.9 us
    all_to_all x8, starting transfers between devices, local(): lax.all_to_all(buckets, 'gy', split_axis=0, concat_axis=0, tiled=True)  58.8 us
    add x8, other arithmetic, local(): displace = displace + TIME_STEP * velocity  54.6 us
    dot_general x8, matrix products, local(): jnp.einsum('pbs,bqs->pbq', state_split, nbr_hot, preferred_element_type=j...  42.5 us
    dot_general x7, matrix products, local(): jnp.einsum('pbq,bqs->pbs', change_split, nbr_hot, preferred_element_type=...  37.9 us
    ppermute x8, starting transfers between devices, laplacian(): yp_face = lax.ppermute(d[:, :, 0], 'gy', shift_pairs('gy', False))  36.6 us
  transfers between devices with their start and end apart: 56, of which 1 were waited for; matrix products, arithmetic and copies ran while one was open for 44% of the time, Pallas kernels for 0%

profile of v1, /device:TPU:38, one launch (start us, length us, event | category | flops | bytes accessed | tf_op | source)
XLA Modules:
  0.0 907.7 jit_solution(9896391537634684495)
XLA Ops:
  10.7 10.9 %gather_fusion.9 = f32[3072,128]{1,0:T(8,128)} fusion(f32[3072,128]{1,0:T(8,128)S(1)} %bitcast.618, s32[3072]{0:T(1024)S(1)} %fusion.241), kind=kCustom, calls=%fused_computation.clone | custom fusion | bytes 3158016 | tf_op jit(solution)/shard_map/jit(_take)/gather | solution.py:118
  24.1 14.1 %gather_fusion = f32[4096,128]{1,0:T(8,128)} fusion(f32[1024,128]{1,0:T(8,128)S(1)} %bitcast.610, s32[4096]{0:T(1024)S(1)} %broadcast_clamp_fusion), kind=kCustom, calls=%fused_computation.16 | custom fusion | bytes 4210688 | tf_op jit(solution)/shard_map/jit(_take)/gather | solution.py:92
  43.4 9.1 %reduce-window.6 = s32[8,16,4,128]{3,1,2,0:T(8,128)S(1)} reduce-window(s32[8,16,4,128]{3,1,2,0:T(8,128)S(1)} %fusion.174, s32[]{:T(128)} %constant.109.clone.1), window={size=1x1x1x128 pad=0_0x0_0x0_0x127_0}, to_apply=%region_1.3 | reduce-window | flops 8323072 | bytes 524292 | tf_op jit(solution)/shard_map/reduce-window
  56.8 8.1 all-to-all-start
  97.0 5.3 fusion.94
  124.0 8.7 all-to-all-start.1
  138.8 5.3 fusion.95
  147.2 18.2 %scatter_custom_fusion.1 = f32[3072,128]{1,0:T(8,128)} fusion(s32[3072]{0:T(1024)} %bitcast.783, f32[3072,128]{1,0:T(8,128)S(1)} %bitcast_select_fusion.14, f32[]{:T(128)} %constant.106.clone.1), kind=kCustom, calls=%fused_computation.240 | custom fusion | flops 393216 | bytes 1573376 | tf_op jit(solution)/shard_map/scatter-add | solution.py:175
  165.5 7.2 multiply_add_fusion.14
  180.6 10.8 %gather_fusion.11 = f32[3072,128]{1,0:T(8,128)} fusion(f32[3072,128]{1,0:T(8,128)S(1)} %bitcast.616, s32[3072]{0:T(1024)S(1)} %fusion.242), kind=kCustom, calls=%fused_computation.2.clone | custom fusion | bytes 3158016 | tf_op jit(solution)/shard_map/jit(_take)/gather | solution.py:118
  203.6 7.2 all-to-all-start.2
  226.0 8.9 all-to-all-start.3
  241.1 5.3 fusion.96
  250.7 18.4 %scatter_custom_fusion.3 = f32[3072,128]{1,0:T(8,128)} fusion(s32[3072]{0:T(1024)} %bitcast.782, f32[3072,128]{1,0:T(8,128)} %bitcast_select_fusion.12, f32[]{:T(128)} %constant.106.clone.1), kind=kCustom, calls=%fused_computation.238 | custom fusion | flops 393216 | bytes 1573376 | tf_op jit(solution)/shard_map/scatter-add | solution.py:175
  269.2 7.2 multiply_add_fusion.12
  284.2 10.9 %gather_fusion.13 = f32[3072,128]{1,0:T(8,128)} fusion(f32[3072,128]{1,0:T(8,128)S(1)} %bitcast.612, s32[3072]{0:T(1024)S(1)} %copy-done.96), kind=kCustom, calls=%fused_computation.3.clone | custom fusion | bytes 3158016 | tf_op jit(solution)/shard_map/jit(_take)/gather | solution.py:118
  311.9 7.2 all-to-all-start.4
  337.6 8.7 all-to-all-start.5
  346.5 6.1 fusion.104
  353.3 5.3 fusion.97
  367.6 18.4 %scatter_custom_fusion.5 = f32[3072,128]{1,0:T(8,128)} fusion(s32[3072]{0:T(1024)} %bitcast.781, f32[3072,128]{1,0:T(8,128)} %bitcast_select_fusion.10, f32[]{:T(128)} %constant.106.clone.1), kind=kCustom, calls=%fused_computation.236 | custom fusion | flops 393216 | bytes 1573376 | tf_op jit(solution)/shard_map/scatter-add | solution.py:175
  386.1 6.6 multiply_add_fusion.10
  400.5 12.3 %gather_fusion.15 = f32[3072,128]{1,0:T(8,128)} fusion(f32[3072,128]{1,0:T(8,128)} %bitcast.613, s32[3072]{0:T(1024)S(1)} %copy-done.95), kind=kCustom, calls=%fused_computation.4.clone | custom fusion | bytes 3158016 | tf_op jit(solution)/shard_map/jit(_take)/gather | solution.py:118
  425.0 7.2 all-to-all-start.6
  447.4 8.7 all-to-all-start.7
  471.9 18.4 %scatter_custom_fusion.7 = f32[3072,128]{1,0:T(8,128)} fusion(s32[3072]{0:T(1024)} %bitcast.780, f32[3072,128]{1,0:T(8,128)} %bitcast_select_fusion.8, f32[]{:T(128)} %constant.106.clone.1), kind=kCustom, calls=%fused_computation.234 | custom fusion | flops 393216 | bytes 1573376 | tf_op jit(solution)/shard_map/scatter-add | solution.py:175
  490.4 6.5 multiply_add_fusion.8
  504.8 12.3 %gather_fusion.17 = f32[3072,128]{1,0:T(8,128)} fusion(f32[3072,128]{1,0:T(8,128)} %bitcast.614, s32[3072]{0:T(1024)S(1)} %copy-done.94), kind=kCustom, calls=%fused_computation.5.clone | custom fusion | bytes 3158016 | tf_op jit(solution)/shard_map/jit(_take)/gather | solution.py:118
  529.3 7.2 all-to-all-start.8
  551.7 8.9 all-to-all-start.9
  575.8 18.4 %scatter_custom_fusion.9 = f32[3072,128]{1,0:T(8,128)} fusion(s32[3072]{0:T(1024)} %bitcast.779, f32[3072,128]{1,0:T(8,128)} %bitcast_select_fusion.6, f32[]{:T(128)} %constant.106.clone.1), kind=kCustom, calls=%fused_computation.232 | custom fusion | flops 393216 | bytes 1573376 | tf_op jit(solution)/shard_map/scatter-add | solution.py:175
  594.3 6.5 multiply_add_fusion.6
  608.7 12.3 %gather_fusion.19 = f32[3072,128]{1,0:T(8,128)} fusion(f32[3072,128]{1,0:T(8,128)} %bitcast.615, s32[3072]{0:T(1024)S(1)} %copy-done.93), kind=kCustom, calls=%fused_computation.6.clone | custom fusion | bytes 3158016 | tf_op jit(solution)/shard_map/jit(_take)/gather | solution.py:118
  633.2 7.2 all-to-all-start.10
  655.6 8.6 all-to-all-start.11
  680.0 18.4 %scatter_custom_fusion.11 = f32[3072,128]{1,0:T(8,128)} fusion(s32[3072]{0:T(1024)} %bitcast.778, f32[3072,128]{1,0:T(8,128)} %bitcast_select_fusion.4, f32[]{:T(128)} %constant.106.clone.1), kind=kCustom, calls=%fused_computation.230 | custom fusion | flops 393216 | bytes 1573376 | tf_op jit(solution)/shard_map/scatter-add | solution.py:175
  698.5 7.2 multiply_add_fusion.4
  713.6 10.9 %gather_fusion.21 = f32[3072,128]{1,0:T(8,128)} fusion(f32[3072,128]{1,0:T(8,128)S(1)} %bitcast.611, s32[3072]{0:T(1024)S(1)} %copy-done.92), kind=kCustom, calls=%fused_computation.7.clone | custom fusion | bytes 3158016 | tf_op jit(solution)/shard_map/jit(_take)/gather | solution.py:118
  736.9 7.2 all-to-all-start.12
  758.1 8.7 all-to-all-start.13
  785.0 18.4 %scatter_custom_fusion.13 = f32[3072,128]{1,0:T(8,128)} fusion(s32[3072]{0:T(1024)} %bitcast.777, f32[3072,128]{1,0:T(8,128)} %bitcast_select_fusion.2, f32[]{:T(128)} %constant.106.clone.1), kind=kCustom, calls=%fused_computation.228 | custom fusion | flops 393216 | bytes 1573376 | tf_op jit(solution)/shard_map/scatter-add | solution.py:175
  803.5 6.6 multiply_add_fusion.2
  817.3 12.3 %gather_fusion.23 = f32[3072,128]{1,0:T(8,128)} fusion(f32[3072,128]{1,0:T(8,128)} %bitcast.617, s32[3072]{0:T(1024)S(1)} %copy-done.91), kind=kCustom, calls=%fused_computation.8.clone | custom fusion | bytes 3158016 | tf_op jit(solution)/shard_map/jit(_take)/gather | solution.py:118
  841.2 7.4 all-to-all-start.14
  861.8 8.7 all-to-all-start.15
  871.2 5.5 all-to-all-done.15
  882.1 18.4 %scatter_custom_fusion.15 = f32[3072,128]{1,0:T(8,128)} fusion(s32[3072]{0:T(1024)} %bitcast.776, f32[3072,128]{1,0:T(8,128)} %bitcast_select_fusion, f32[]{:T(128)} %constant.106.clone.1), kind=kCustom, calls=%fused_computation.226 | custom fusion | flops 393216 | bytes 1573376 | tf_op jit(solution)/shard_map/scatter-add | solution.py:175
  900.6 6.7 multiply_add_fusion
  (916 shorter events, 423.3 us)
Async XLA Ops:
  56.8 65.3 %all-to-all-start = ((f32[16,128,8]{1,2,0:T(8,128)}), f32[16,128,8]{1,2,0:T(8,128)S(1)}, u32[]{:S(2)}, u32[]{:S(2)}) async-start(f32[16,128,8]{1,2,0:T(8,128)} %copy.186), calls=%async_computation | async-start | bytes 131072 | tf_op jit(solution)/shard_map/all_to_all | solution.py:138
  64.9 56.6 %collective-permute-start.4 = (f32[3,512]{1,0:T(4,128)}, f32[3,512]{1,0:T(4,128)S(1)}, u32[]{:S(2)}, u32[]{:S(2)}) collective-permute-start(f32[3,512]{1,0:T(4,128)} %get-tuple-element.269), channel_id=1, source_target_pairs={{0,16},{16,0},{32,48},{48,32},{64,80},{80,64},{96,112},{112,96},{1... | collective-permute-start | bytes 18440 | tf_op jit(solution)/shard_map/ppermute | solution.py:23
  65.5 99.9 %collective-permute-start = (f32[3,32,128]{2,1,0:T(8,128)}, f32[3,32,128]{2,1,0:T(8,128)S(1)}, u32[]{:S(2)}, u32[]{:S(2)}) collective-permute-start(f32[3,32,128]{2,1,0:T(8,128)} %get-tuple-element.108), channel_id=1, source_target_pairs={{16,0},{32,16},{48,32},{64,48},{80,64},{96,80},{112,96},{17,1},{33... | collective-permute-start | bytes 147464 | tf_op jit(solution)/shard_map/ppermute | solution.py:36
  68.4 97.1 %collective-permute-start.1 = (f32[3,32,128]{2,1,0:T(8,128)}, f32[3,32,128]{2,1,0:T(8,128)S(1)}, u32[]{:S(2)}, u32[]{:S(2)}) collective-permute-start(f32[3,32,128]{2,1,0:T(8,128)} %get-tuple-element.109), channel_id=1, source_target_pairs={{0,16},{16,32},{32,48},{48,64},{64,80},{80,96},{96,112},{1,17},{17... | collective-permute-start | bytes 147464 | tf_op jit(solution)/shard_map/ppermute | solution.py:35
  71.0 94.4 %collective-permute-start.2 = (f32[3,32,128]{2,1,0:T(8,128)}, f32[3,32,128]{2,1,0:T(8,128)}, u32[]{:S(2)}, u32[]{:S(2)}) collective-permute-start(f32[3,32,128]{2,1,0:T(8,128)} %bitcast.4), channel_id=1, source_target_pairs={{1,0},{2,1},{3,2},{4,3},{5,4},{6,5},{7,6},{8,7},{9,8},{10,9},{11,1... | collective-permute-start | bytes 147464 | tf_op jit(solution)/shard_map/ppermute | solution.py:38
  75.6 89.9 %collective-permute-start.3 = (f32[3,32,128]{2,1,0:T(8,128)}, f32[3,32,128]{2,1,0:T(8,128)}, u32[]{:S(2)}, u32[]{:S(2)}) collective-permute-start(f32[3,32,128]{2,1,0:T(8,128)} %bitcast.6), channel_id=1, source_target_pairs={{0,1},{1,2},{2,3},{3,4},{4,5},{5,6},{6,7},{7,8},{8,9},{9,10},{10,1... | collective-permute-start | bytes 147464 | tf_op jit(solution)/shard_map/ppermute | solution.py:37
  124.0 21.2 %all-to-all-start.1 = ((f32[16,128,3]{1,2,0:T(4,128)}), f32[16,128,3]{1,2,0:T(4,128)S(1)}, u32[]{:S(2)}, u32[]{:S(2)}) async-start(f32[16,128,3]{1,2,0:T(4,128)} %copy.190), calls=%async_computation.1 | async-start | bytes 65536 | tf_op jit(solution)/shard_map/all_to_all | solution.py:160
  194.5 27.8 %collective-permute-start.9 = (f32[3,512]{1,0:T(4,128)}, f32[3,512]{1,0:T(4,128)}, u32[]{:S(2)}, u32[]{:S(2)}) collective-permute-start(f32[3,512]{1,0:T(4,128)} %get-tuple-element.267), channel_id=1, source_target_pairs={{0,16},{16,0},{32,48},{48,32},{64,80},{80,64},{96,112},{112,96},{1... | collective-permute-start | bytes 18440 | tf_op jit(solution)/shard_map/ppermute | solution.py:23
  210.8 58.3 %collective-permute-start.5 = (f32[3,32,128]{2,1,0:T(8,128)}, f32[3,32,128]{2,1,0:T(8,128)}, u32[]{:S(2)}, u32[]{:S(2)}) collective-permute-start(f32[3,32,128]{2,1,0:T(8,128)} %get-tuple-element.98), channel_id=1, source_target_pairs={{16,0},{32,16},{48,32},{64,48},{80,64},{96,80},{112,96},{17,1},{33... | collective-permute-start | bytes 147464 | tf_op jit(solution)/shard_map/ppermute | solution.py:36
  212.8 56.3 %collective-permute-start.6 = (f32[3,32,128]{2,1,0:T(8,128)}, f32[3,32,128]{2,1,0:T(8,128)}, u32[]{:S(2)}, u32[]{:S(2)}) collective-permute-start(f32[3,32,128]{2,1,0:T(8,128)} %get-tuple-element.99), channel_id=1, source_target_pairs={{0,16},{16,32},{32,48},{48,64},{64,80},{80,96},{96,112},{1,17},{17... | collective-permute-start | bytes 147464 | tf_op jit(solution)/shard_map/ppermute | solution.py:35
  215.8 53.4 %collective-permute-start.7 = (f32[3,32,128]{2,1,0:T(8,128)}, f32[3,32,128]{2,1,0:T(8,128)}, u32[]{:S(2)}, u32[]{:S(2)}) collective-permute-start(f32[3,32,128]{2,1,0:T(8,128)} %bitcast.45), channel_id=1, source_target_pairs={{1,0},{2,1},{3,2},{4,3},{5,4},{6,5},{7,6},{8,7},{9,8},{10,9},{11,1... | collective-permute-start | bytes 147464 | tf_op jit(solution)/shard_map/ppermute | solution.py:38
  220.3 48.8 %collective-permute-start.8 = (f32[3,32,128]{2,1,0:T(8,128)}, f32[3,32,128]{2,1,0:T(8,128)}, u32[]{:S(2)}, u32[]{:S(2)}) collective-permute-start(f32[3,32,128]{2,1,0:T(8,128)} %bitcast.47), channel_id=1, source_target_pairs={{0,1},{1,2},{2,3},{3,4},{4,5},{5,6},{6,7},{7,8},{8,9},{9,10},{10,1... | collective-permute-start | bytes 147464 | tf_op jit(solution)/shard_map/ppermute | solution.py:37
  226.0 21.5 %all-to-all-start.3 = ((f32[16,128,3]{1,2,0:T(4,128)}), f32[16,128,3]{1,2,0:T(4,128)S(1)}, u32[]{:S(2)}, u32[]{:S(2)}) async-start(f32[16,128,3]{1,2,0:T(4,128)} %copy.208), calls=%async_computation.3 | async-start | bytes 65536 | tf_op jit(solution)/shard_map/all_to_all | solution.py:160
  298.1 32.4 %collective-permute-start.14 = (f32[3,512]{1,0:T(4,128)}, f32[3,512]{1,0:T(4,128)}, u32[]{:S(2)}, u32[]{:S(2)}) collective-permute-start(f32[3,512]{1,0:T(4,128)} %get-tuple-element.265), channel_id=1, source_target_pairs={{0,16},{16,0},{32,48},{48,32},{64,80},{80,64},{96,112},{112,96},{1... | collective-permute-start | bytes 18440 | tf_op jit(solution)/shard_map/ppermute | solution.py:23
  319.1 66.9 %collective-permute-start.10 = (f32[3,32,128]{2,1,0:T(8,128)}, f32[3,32,128]{2,1,0:T(8,128)}, u32[]{:S(2)}, u32[]{:S(2)}) collective-permute-start(f32[3,32,128]{2,1,0:T(8,128)} %get-tuple-element.88), channel_id=1, source_target_pairs={{16,0},{32,16},{48,32},{64,48},{80,64},{96,80},{112,96},{17,1},{33... | collective-permute-start | bytes 147464 | tf_op jit(solution)/shard_map/ppermute | solution.py:36
  321.0 65.0 %collective-permute-start.11 = (f32[3,32,128]{2,1,0:T(8,128)}, f32[3,32,128]{2,1,0:T(8,128)}, u32[]{:S(2)}, u32[]{:S(2)}) collective-permute-start(f32[3,32,128]{2,1,0:T(8,128)} %get-tuple-element.89), channel_id=1, source_target_pairs={{0,16},{16,32},{32,48},{48,64},{64,80},{80,96},{96,112},{1,17},{17... | collective-permute-start | bytes 147464 | tf_op jit(solution)/shard_map/ppermute | solution.py:35
  324.0 62.0 %collective-permute-start.12 = (f32[3,32,128]{2,1,0:T(8,128)}, f32[3,32,128]{2,1,0:T(8,128)}, u32[]{:S(2)}, u32[]{:S(2)}) collective-permute-start(f32[3,32,128]{2,1,0:T(8,128)} %bitcast.80), channel_id=1, source_target_pairs={{1,0},{2,1},{3,2},{4,3},{5,4},{6,5},{7,6},{8,7},{9,8},{10,9},{11,1... | collective-permute-start | bytes 147464 | tf_op jit(solution)/shard_map/ppermute | solution.py:38
  328.6 57.4 %collective-permute-start.13 = (f32[3,32,128]{2,1,0:T(8,128)}, f32[3,32,128]{2,1,0:T(8,128)}, u32[]{:S(2)}, u32[]{:S(2)}) collective-permute-start(f32[3,32,128]{2,1,0:T(8,128)} %bitcast.82), channel_id=1, source_target_pairs={{0,1},{1,2},{2,3},{3,4},{4,5},{5,6},{6,7},{7,8},{8,9},{9,10},{10,1... | collective-permute-start | bytes 147464 | tf_op jit(solution)/shard_map/ppermute | solution.py:37
  337.6 23.8 %all-to-all-start.5 = ((f32[16,128,3]{1,2,0:T(4,128)}), f32[16,128,3]{1,2,0:T(4,128)}, u32[]{:S(2)}, u32[]{:S(2)}) async-start(f32[16,128,3]{1,2,0:T(4,128)} %copy.224), calls=%async_computation.5 | async-start | bytes 65536 | tf_op jit(solution)/shard_map/all_to_all | solution.py:160
  415.9 27.8 %collective-permute-start.19 = (f32[3,512]{1,0:T(4,128)}, f32[3,512]{1,0:T(4,128)}, u32[]{:S(2)}, u32[]{:S(2)}) collective-permute-start(f32[3,512]{1,0:T(4,128)} %get-tuple-element.263), channel_id=1, source_target_pairs={{0,16},{16,0},{32,48},{48,32},{64,80},{80,64},{96,112},{112,96},{1... | collective-permute-start | bytes 18440 | tf_op jit(solution)/shard_map/ppermute | solution.py:23
  432.2 58.1 %collective-permute-start.15 = (f32[3,32,128]{2,1,0:T(8,128)}, f32[3,32,128]{2,1,0:T(8,128)}, u32[]{:S(2)}, u32[]{:S(2)}) collective-permute-start(f32[3,32,128]{2,1,0:T(8,128)} %get-tuple-element.78), channel_id=1, source_target_pairs={{16,0},{32,16},{48,32},{64,48},{80,64},{96,80},{112,96},{17,1},{33... | collective-permute-start | bytes 147464 | tf_op jit(solution)/shard_map/ppermute | solution.py:36
  434.1 56.2 %collective-permute-start.16 = (f32[3,32,128]{2,1,0:T(8,128)}, f32[3,32,128]{2,1,0:T(8,128)}, u32[]{:S(2)}, u32[]{:S(2)}) collective-permute-start(f32[3,32,128]{2,1,0:T(8,128)} %get-tuple-element.79), channel_id=1, source_target_pairs={{0,16},{16,32},{32,48},{48,64},{64,80},{80,96},{96,112},{1,17},{17... | collective-permute-start | bytes 147464 | tf_op jit(solution)/shard_map/ppermute | solution.py:35
  437.1 53.2 %collective-permute-start.17 = (f32[3,32,128]{2,1,0:T(8,128)}, f32[3,32,128]{2,1,0:T(8,128)}, u32[]{:S(2)}, u32[]{:S(2)}) collective-permute-start(f32[3,32,128]{2,1,0:T(8,128)} %bitcast.113), channel_id=1, source_target_pairs={{1,0},{2,1},{3,2},{4,3},{5,4},{6,5},{7,6},{8,7},{9,8},{10,9},{11,1... | collective-permute-start | bytes 147464 | tf_op jit(solution)/shard_map/ppermute | solution.py:38
  441.7 48.6 %collective-permute-start.18 = (f32[3,32,128]{2,1,0:T(8,128)}, f32[3,32,128]{2,1,0:T(8,128)}, u32[]{:S(2)}, u32[]{:S(2)}) collective-permute-start(f32[3,32,128]{2,1,0:T(8,128)} %bitcast.115), channel_id=1, source_target_pairs={{0,1},{1,2},{2,3},{3,4},{4,5},{5,6},{6,7},{7,8},{8,9},{9,10},{10,1... | collective-permute-start | bytes 147464 | tf_op jit(solution)/shard_map/ppermute | solution.py:37
  447.4 21.3 %all-to-all-start.7 = ((f32[16,128,3]{1,2,0:T(4,128)}), f32[16,128,3]{1,2,0:T(4,128)S(1)}, u32[]{:S(2)}, u32[]{:S(2)}) async-start(f32[16,128,3]{1,2,0:T(4,128)} %copy.240), calls=%async_computation.7 | async-start | bytes 65536 | tf_op jit(solution)/shard_map/all_to_all | solution.py:160
  520.1 27.8 %collective-permute-start.24 = (f32[3,512]{1,0:T(4,128)}, f32[3,512]{1,0:T(4,128)}, u32[]{:S(2)}, u32[]{:S(2)}) collective-permute-start(f32[3,512]{1,0:T(4,128)} %get-tuple-element.261), channel_id=1, source_target_pairs={{0,16},{16,0},{32,48},{48,32},{64,80},{80,64},{96,112},{112,96},{1... | collective-permute-start | bytes 18440 | tf_op jit(solution)/shard_map/ppermute | solution.py:23
  536.5 57.8 %collective-permute-start.20 = (f32[3,32,128]{2,1,0:T(8,128)}, f32[3,32,128]{2,1,0:T(8,128)}, u32[]{:S(2)}, u32[]{:S(2)}) collective-permute-start(f32[3,32,128]{2,1,0:T(8,128)} %get-tuple-element.68), channel_id=1, source_target_pairs={{16,0},{32,16},{48,32},{64,48},{80,64},{96,80},{112,96},{17,1},{33... | collective-permute-start | bytes 147464 | tf_op jit(solution)/shard_map/ppermute | solution.py:36
  538.4 55.9 %collective-permute-start.21 = (f32[3,32,128]{2,1,0:T(8,128)}, f32[3,32,128]{2,1,0:T(8,128)}, u32[]{:S(2)}, u32[]{:S(2)}) collective-permute-start(f32[3,32,128]{2,1,0:T(8,128)} %get-tuple-element.69), channel_id=1, source_target_pairs={{0,16},{16,32},{32,48},{48,64},{64,80},{80,96},{96,112},{1,17},{17... | collective-permute-start | bytes 147464 | tf_op jit(solution)/shard_map/ppermute | solution.py:35
  541.4 52.9 %collective-permute-start.22 = (f32[3,32,128]{2,1,0:T(8,128)}, f32[3,32,128]{2,1,0:T(8,128)}, u32[]{:S(2)}, u32[]{:S(2)}) collective-permute-start(f32[3,32,128]{2,1,0:T(8,128)} %bitcast.146), channel_id=1, source_target_pairs={{1,0},{2,1},{3,2},{4,3},{5,4},{6,5},{7,6},{8,7},{9,8},{10,9},{11,1... | collective-permute-start | bytes 147464 | tf_op jit(solution)/shard_map/ppermute | solution.py:38
  546.0 48.3 %collective-permute-start.23 = (f32[3,32,128]{2,1,0:T(8,128)}, f32[3,32,128]{2,1,0:T(8,128)}, u32[]{:S(2)}, u32[]{:S(2)}) collective-permute-start(f32[3,32,128]{2,1,0:T(8,128)} %bitcast.148), channel_id=1, source_target_pairs={{0,1},{1,2},{2,3},{3,4},{4,5},{5,6},{6,7},{7,8},{8,9},{9,10},{10,1... | collective-permute-start | bytes 147464 | tf_op jit(solution)/shard_map/ppermute | solution.py:37
  551.7 20.9 %all-to-all-start.9 = ((f32[16,128,3]{1,2,0:T(4,128)}), f32[16,128,3]{1,2,0:T(4,128)S(1)}, u32[]{:S(2)}, u32[]{:S(2)}) async-start(f32[16,128,3]{1,2,0:T(4,128)} %copy.256), calls=%async_computation.9 | async-start | bytes 65536 | tf_op jit(solution)/shard_map/all_to_all | solution.py:160
  624.1 27.8 %collective-permute-start.29 = (f32[3,512]{1,0:T(4,128)}, f32[3,512]{1,0:T(4,128)}, u32[]{:S(2)}, u32[]{:S(2)}) collective-permute-start(f32[3,512]{1,0:T(4,128)} %get-tuple-element.259), channel_id=1, source_target_pairs={{0,16},{16,0},{32,48},{48,32},{64,80},{80,64},{96,112},{112,96},{1... | collective-permute-start | bytes 18440 | tf_op jit(solution)/shard_map/ppermute | solution.py:23
  640.4 58.1 %collective-permute-start.25 = (f32[3,32,128]{2,1,0:T(8,128)}, f32[3,32,128]{2,1,0:T(8,128)}, u32[]{:S(2)}, u32[]{:S(2)}) collective-permute-start(f32[3,32,128]{2,1,0:T(8,128)} %get-tuple-element.58), channel_id=1, source_target_pairs={{16,0},{32,16},{48,32},{64,48},{80,64},{96,80},{112,96},{17,1},{33... | collective-permute-start | bytes 147464 | tf_op jit(solution)/shard_map/ppermute | solution.py:36
  642.3 56.2 %collective-permute-start.26 = (f32[3,32,128]{2,1,0:T(8,128)}, f32[3,32,128]{2,1,0:T(8,128)}, u32[]{:S(2)}, u32[]{:S(2)}) collective-permute-start(f32[3,32,128]{2,1,0:T(8,128)} %get-tuple-element.59), channel_id=1, source_target_pairs={{0,16},{16,32},{32,48},{48,64},{64,80},{80,96},{96,112},{1,17},{17... | collective-permute-start | bytes 147464 | tf_op jit(solution)/shard_map/ppermute | solution.py:35
  645.4 53.2 %collective-permute-start.27 = (f32[3,32,128]{2,1,0:T(8,128)}, f32[3,32,128]{2,1,0:T(8,128)}, u32[]{:S(2)}, u32[]{:S(2)}) collective-permute-start(f32[3,32,128]{2,1,0:T(8,128)} %bitcast.179), channel_id=1, source_target_pairs={{1,0},{2,1},{3,2},{4,3},{5,4},{6,5},{7,6},{8,7},{9,8},{10,9},{11,1... | collective-permute-start | bytes 147464 | tf_op jit(solution)/shard_map/ppermute | solution.py:38
  649.9 48.6 %collective-permute-start.28 = (f32[3,32,128]{2,1,0:T(8,128)}, f32[3,32,128]{2,1,0:T(8,128)}, u32[]{:S(2)}, u32[]{:S(2)}) collective-permute-start(f32[3,32,128]{2,1,0:T(8,128)} %bitcast.181), channel_id=1, source_target_pairs={{0,1},{1,2},{2,3},{3,4},{4,5},{5,6},{6,7},{7,8},{8,9},{9,10},{10,1... | collective-permute-start | bytes 147464 | tf_op jit(solution)/shard_map/ppermute | solution.py:37
  655.6 21.2 %all-to-all-start.11 = ((f32[16,128,3]{1,2,0:T(4,128)}), f32[16,128,3]{1,2,0:T(4,128)S(1)}, u32[]{:S(2)}, u32[]{:S(2)}) async-start(f32[16,128,3]{1,2,0:T(4,128)} %copy.272), calls=%async_computation.11 | async-start | bytes 65536 | tf_op jit(solution)/shard_map/all_to_all | solution.py:160
  726.9 28.7 %collective-permute-start.34 = (f32[3,512]{1,0:T(4,128)S(1)}, f32[3,512]{1,0:T(4,128)S(1)}, u32[]{:S(2)}, u32[]{:S(2)}) collective-permute-start(f32[3,512]{1,0:T(4,128)S(1)} %get-tuple-element.257), channel_id=1, source_target_pairs={{0,16},{16,0},{32,48},{48,32},{64,80},{80,64},{96,112},{112,96},{1... | collective-permute-start | bytes 18440 | tf_op jit(solution)/shard_map/ppermute | solution.py:23
  744.2 59.3 %collective-permute-start.30 = (f32[3,32,128]{2,1,0:T(8,128)}, f32[3,32,128]{2,1,0:T(8,128)}, u32[]{:S(2)}, u32[]{:S(2)}) collective-permute-start(f32[3,32,128]{2,1,0:T(8,128)} %get-tuple-element.48), channel_id=1, source_target_pairs={{16,0},{32,16},{48,32},{64,48},{80,64},{96,80},{112,96},{17,1},{33... | collective-permute-start | bytes 147464 | tf_op jit(solution)/shard_map/ppermute | solution.py:36
  746.1 57.4 %collective-permute-start.31 = (f32[3,32,128]{2,1,0:T(8,128)}, f32[3,32,128]{2,1,0:T(8,128)}, u32[]{:S(2)}, u32[]{:S(2)}) collective-permute-start(f32[3,32,128]{2,1,0:T(8,128)} %get-tuple-element.49), channel_id=1, source_target_pairs={{0,16},{16,32},{32,48},{48,64},{64,80},{80,96},{96,112},{1,17},{17... | collective-permute-start | bytes 147464 | tf_op jit(solution)/shard_map/ppermute | solution.py:35
  749.1 54.4 %collective-permute-start.32 = (f32[3,32,128]{2,1,0:T(8,128)}, f32[3,32,128]{2,1,0:T(8,128)}, u32[]{:S(2)}, u32[]{:S(2)}) collective-permute-start(f32[3,32,128]{2,1,0:T(8,128)} %bitcast.212), channel_id=1, source_target_pairs={{1,0},{2,1},{3,2},{4,3},{5,4},{6,5},{7,6},{8,7},{9,8},{10,9},{11,1... | collective-permute-start | bytes 147464 | tf_op jit(solution)/shard_map/ppermute | solution.py:38
  753.7 49.8 %collective-permute-start.33 = (f32[3,32,128]{2,1,0:T(8,128)}, f32[3,32,128]{2,1,0:T(8,128)}, u32[]{:S(2)}, u32[]{:S(2)}) collective-permute-start(f32[3,32,128]{2,1,0:T(8,128)} %bitcast.214), channel_id=1, source_target_pairs={{0,1},{1,2},{2,3},{3,4},{4,5},{5,6},{6,7},{7,8},{8,9},{9,10},{10,1... | collective-permute-start | bytes 147464 | tf_op jit(solution)/shard_map/ppermute | solution.py:37
  758.1 20.8 %all-to-all-start.13 = ((f32[16,128,3]{1,2,0:T(4,128)}), f32[16,128,3]{1,2,0:T(4,128)}, u32[]{:S(2)}, u32[]{:S(2)}) async-start(f32[16,128,3]{1,2,0:T(4,128)} %copy.288), calls=%async_computation.13 | async-start | bytes 65536 | tf_op jit(solution)/shard_map/all_to_all | solution.py:160
  849.2 21.4 %collective-permute-start.39 = (f32[3,512]{1,0:T(4,128)}, f32[3,512]{1,0:T(4,128)S(1)}, u32[]{:S(2)}, u32[]{:S(2)}) collective-permute-start(f32[3,512]{1,0:T(4,128)} %get-tuple-element.231), channel_id=1, source_target_pairs={{0,16},{16,0},{32,48},{48,32},{64,80},{80,64},{96,112},{112,96},{1... | collective-permute-start | bytes 18440 | tf_op jit(solution)/shard_map/ppermute | solution.py:23
  849.2 51.4 %collective-permute-start.35 = (f32[3,32,128]{2,1,0:T(8,128)}, f32[3,32,128]{2,1,0:T(8,128)S(1)}, u32[]{:S(2)}, u32[]{:S(2)}) collective-permute-start(f32[3,32,128]{2,1,0:T(8,128)} %get-tuple-element.38), channel_id=1, source_target_pairs={{16,0},{32,16},{48,32},{64,48},{80,64},{96,80},{112,96},{17,1},{33... | collective-permute-start | bytes 147464 | tf_op jit(solution)/shard_map/ppermute | solution.py:36
  851.1 49.5 %collective-permute-start.36 = (f32[3,32,128]{2,1,0:T(8,128)}, f32[3,32,128]{2,1,0:T(8,128)S(1)}, u32[]{:S(2)}, u32[]{:S(2)}) collective-permute-start(f32[3,32,128]{2,1,0:T(8,128)} %get-tuple-element.39), channel_id=1, source_target_pairs={{0,16},{16,32},{32,48},{48,64},{64,80},{80,96},{96,112},{1,17},{17... | collective-permute-start | bytes 147464 | tf_op jit(solution)/shard_map/ppermute | solution.py:35
  853.5 47.1 %collective-permute-start.37 = (f32[3,32,128]{2,1,0:T(8,128)}, f32[3,32,128]{2,1,0:T(8,128)}, u32[]{:S(2)}, u32[]{:S(2)}) collective-permute-start(f32[3,32,128]{2,1,0:T(8,128)} %bitcast.245), channel_id=1, source_target_pairs={{1,0},{2,1},{3,2},{4,3},{5,4},{6,5},{7,6},{8,7},{9,8},{10,9},{11,1... | collective-permute-start | bytes 147464 | tf_op jit(solution)/shard_map/ppermute | solution.py:38
  858.1 42.5 %collective-permute-start.38 = (f32[3,32,128]{2,1,0:T(8,128)}, f32[3,32,128]{2,1,0:T(8,128)}, u32[]{:S(2)}, u32[]{:S(2)}) collective-permute-start(f32[3,32,128]{2,1,0:T(8,128)} %bitcast.247), channel_id=1, source_target_pairs={{0,1},{1,2},{2,3},{3,4},{4,5},{5,6},{6,7},{7,8},{8,9},{9,10},{10,1... | collective-permute-start | bytes 147464 | tf_op jit(solution)/shard_map/ppermute | solution.py:37
  (165 other events, 2202.0 us)

commit v2 on v0

--- a/solution.py
+++ b/solution.py
@@ -31,6 +31,14 @@
     mask = 2**stride
     pairs = [(source, source ^ mask) for source in range(lax.axis_size(axis))]
     return lax.ppermute(value, axis, pairs)
+
+
+def split3(x):
+    hi = lax.reduce_precision(x, exponent_bits=8, mantissa_bits=7)
+    rest = x - hi
+    mid = lax.reduce_precision(rest, exponent_bits=8, mantissa_bits=7)
+    lo = rest - mid
+    return jnp.stack([hi, mid, lo]).astype(jnp.bfloat16)
 
 
 def depth_sum(field):
@@ -72,11 +80,19 @@
         contact_match[0, 0][:, None] == jnp.arange(n_seg, dtype=jnp.int32)[None, :]
     ).astype(jnp.float32)
     local_nbr = bed_neighbours[0, 0].reshape(n_nbr, n_blocks, row_block).transpose(1, 0, 2)
-    nbr_hot = (local_nbr[..., None] == jnp.arange(row_block, dtype=jnp.int32)).astype(jnp.float32)
-    rec_range = jnp.arange(n_rec, dtype=jnp.int32)
-    lower_tri = (rec_range[None, :] <= rec_range[:, None]).astype(jnp.float32)
+    nbr_hot = (
+        local_nbr.reshape(n_blocks, n_nbr * row_block)[..., None]
+        == jnp.arange(row_block, dtype=jnp.int32)
+    ).astype(jnp.bfloat16)
+    nbr_hot = lax.optimization_barrier(nbr_hot)
     owner_range = jnp.arange(n_owner, dtype=jnp.int32)
-    rank_range = jnp.arange(capacity, dtype=jnp.float32)
+    rank_range = jnp.arange(capacity, dtype=jnp.int32)
+    owners_all = owner_ids[:, 0, 0, :, 0]
+    owner_hit = owners_all[..., None] == owner_range
+    counted_all = jnp.cumsum(owner_hit.astype(jnp.int32), axis=1)
+    rank_all = jnp.sum(jnp.where(owner_hit, counted_all, 0), axis=-1) - 1
+    is_owner_all = owner_hit.astype(jnp.float32)
+    rank_hot_all = (rank_all[..., None] == rank_range).astype(jnp.float32)
     mass_cols = cell_mass.reshape(n_cols, layers)
     part_pos = bed_position[0, 0]
     part_vel = bed_velocity[0, 0]
@@ -101,7 +117,6 @@
         )
         forces = forces.at[:, :, layers - 1].add(top_add)
         cells_now = eroded_cells[step_id, 0, 0]
-        owners_now = owner_ids[step_id, 0, 0, :, 0]
         col_hot = ((cells_now // layers)[:, None] == col_range[None, :]).astype(jnp.float32)
         layer_hot = ((cells_now % layers)[:, None] == layer_range[None, :]).astype(jnp.float32)
         stacked = jnp.concatenate([mass_cols[None], disp_cols, vel_cols], axis=0)
@@ -110,18 +125,17 @@
         rec_mass = picked[0]
         rec_disp = picked[1:4]
         rec_mom = rec_mass[None] * picked[4:7]
-        is_owner = (owners_now[:, None] == owner_range[None, :]).astype(jnp.float32)
-        counted = jnp.dot(lower_tri, is_owner, precision=HIGHEST)
-        rank_value = jnp.sum(is_owner * counted, axis=1) - 1.0
-        rank_hot = (rank_value[:, None] == rank_range[None, :]).astype(jnp.float32)
-        pos_blocks = part_pos.reshape(3, n_blocks, row_block)
-        drift_blocks = part_vel.reshape(3, n_blocks, row_block)
-        bed_near = jnp.einsum("fbs,bkrs->fkbr", pos_blocks, nbr_hot, precision=HIGHEST).reshape(
-            3, n_nbr, n_slots
-        )
-        bed_drift = jnp.einsum("fbs,bkrs->fkbr", drift_blocks, nbr_hot, precision=HIGHEST).reshape(
-            3, n_nbr, n_slots
-        )
+        is_owner = is_owner_all[step_id]
+        rank_hot = rank_hot_all[step_id]
+        state = jnp.concatenate([part_pos, part_vel], axis=0).reshape(6, n_blocks, row_block)
+        state_split = split3(state).reshape(3 * 6, n_blocks, row_block)
+        gathered = jnp.einsum(
+            "pbs,bqs->pbq", state_split, nbr_hot, preferred_element_type=jnp.float32
+        ).reshape(3, 6, n_blocks, n_nbr, row_block)
+        gathered = gathered[0] + gathered[1] + gathered[2]
+        gathered = gathered.transpose(0, 2, 1, 3).reshape(6, n_nbr, n_slots)
+        bed_near = gathered[0:3]
+        bed_drift = gathered[3:6]
         records = jnp.concatenate([rec_mass[None], rec_disp, rec_mom], axis=0)
         buckets = jnp.einsum("eo,fe,er->ofr", is_owner, records, rank_hot, precision=HIGHEST)
         arrived = lax.all_to_all(buckets, "gy", split_axis=0, concat_axis=0, tiled=True)
@@ -138,9 +152,12 @@
         answers = lax.all_to_all(returned, "gy", split_axis=0, concat_axis=0, tiled=True)
         rec_force = jnp.einsum("ofr,er,eo->fe", answers, rank_hot, is_owner, precision=HIGHEST)
         change = (-TIME_STEP * spring / n_nbr).reshape(3, n_nbr, n_blocks, row_block)
-        vel_add = jnp.einsum("fkbr,bkrs->fbs", change, nbr_hot, precision=HIGHEST).reshape(
-            3, n_slots
-        )
+        change = change.transpose(0, 2, 1, 3).reshape(3, n_blocks, n_nbr * row_block)
+        change_split = split3(change).reshape(9, n_blocks, n_nbr * row_block)
+        vel_add = jnp.einsum(
+            "pbq,bqs->pbs", change_split, nbr_hot, preferred_element_type=jnp.float32
+        ).reshape(3, 3, n_slots)
+        vel_add = vel_add[0] + vel_add[1] + vel_add[2]
         part_vel = part_vel + vel_add
         part_pos = part_pos + TIME_STEP * part_vel
         rec_add = jnp.einsum("ec,fe,ez->fcz", col_hot, rec_force, layer_hot, precision=HIGHEST)

time: 728 us -> 674 us (0.926)
  matrix products: 221 us -> 140 us
  other arithmetic: 97.8 us -> 117 us
  local copies, waits for them, and re-layouts: 164 us -> 173 us
  waiting for transfers between devices: 19.4 us -> 11.4 us
    dot_general x31 -> x15, matrix products: 136 us -> 39.9 us  [the longest x7 21.6 us: local(): jnp.einsum('pbq,bqs->pbs', change_split, nbr_hot, preferred_element_type=...]
    another operation x16 -> x41, other arithmetic: 6.3 us -> 16.2 us
    dot_general x8, matrix products: 5.34 us -> 12.8 us  [local(): jnp.einsum('ofr,er,eo->fe', answers, rank_hot, is_owner, precision=HIGHEST)]
    unnamed x202 -> x230, local copies, waits for them, and re-layouts: 27.4 us -> 34 us
  transfers between devices with their start and end apart: 56 -> 56, of which waited for: 15 -> 8; matrix products, arithmetic and copies ran while one was open for 27% -> 18% of each run, Pallas kernels for 0% -> 0%
where the time goes in v2:
time: 674 us; the launch traced here: 661 us
  starting transfers between devices  215 us (32%)
  local copies, waits for them, and re-layouts  173 us (26%)
  matrix products  140 us (21%)
  other arithmetic  117 us (17%)
  waiting for transfers between devices  11.4 us (2%)
    all_to_all x8, starting transfers between devices, local(): lax.all_to_all(returned, 'gy', split_axis=0, concat_axis=0, tiled=True)  68.1 us
    all_to_all x8, starting transfers between devices, local(): lax.all_to_all(buckets, 'gy', split_axis=0, concat_axis=0, tiled=True)  58.6 us
    ppermute x16, starting transfers between devices, padded_2(): lax.ppermute(head, axis, [((i + 1) % count, i) for i in range(ends)])  53.6 us
    ppermute x16, starting transfers between devices, padded_2(): lax.ppermute(tail, axis, [(i, (i + 1) % count) for i in range(ends)])  34.8 us
    unnamed x230, local copies, waits for them, and re-layouts  34 us
    add x8, other arithmetic, local(): displace = displace + TIME_STEP * velocity  31.2 us
    mul x8, other arithmetic, local(): internal = stiffness[None] * laplace  29.7 us
    dot_general x8, matrix products, local(): jnp.einsum('ec,fe,ez->fcz', col_hot, rec_force, layer_hot, precision=HIGH...  29.3 us
  transfers between devices with their start and end apart: 56, of which 8 were waited for; matrix products, arithmetic and copies ran while one was open for 18% of the time, Pallas kernels for 0%

profile of v2, /device:TPU:38, one launch (start us, length us, event | category | flops | bytes accessed | tf_op | source)
XLA Modules:
  0.0 660.9 jit_solution(5269126672368391923)
XLA Ops:
  13.9 9.1 %reduce-window.6 = s32[8,16,4,128]{3,1,2,0:T(8,128)S(1)} reduce-window(s32[8,16,4,128]{3,1,2,0:T(8,128)S(1)} %fusion.220, s32[]{:T(128)} %constant.315.clone.1), window={size=1x1x1x128 pad=0_0x0_0x0_0x127_0}, to_apply=%region_0.0 | reduce-window | flops 8323072 | bytes 524292 | tf_op jit(solution)/shard_map/reduce-window
  26.3 8.1 %all-to-all-start = ((f32[16,7,128]{2,1,0:T(8,128)}), f32[16,7,128]{2,1,0:T(8,128)S(1)}, u32[]{:S(2)}, u32[]{:S(2)}) async-start(f32[16,7,128]{2,1,0:T(8,128)} %copy.319), calls=%async_computation | async-start | bytes 131072 | tf_op jit(solution)/shard_map/all_to_all | solution.py:141
  63.4 4.6 collective-permute-start.2
  72.1 8.4 %all-to-all-start.1 = ((f32[16,3,128]{2,1,0:T(4,128)}), f32[16,3,128]{2,1,0:T(4,128)}, u32[]{:S(2)}, u32[]{:S(2)}) async-start(f32[16,3,128]{2,1,0:T(4,128)} %copy.323), calls=%async_computation.1 | async-start | bytes 65536 | tf_op jit(solution)/shard_map/all_to_all | solution.py:152
  88.8 3.9 fusion.102
  100.2 3.8 bitcast_add_fusion.7
  107.1 3.9 multiply_add_fusion.14
  127.4 7.2 %all-to-all-start.2 = ((f32[16,7,128]{2,1,0:T(8,128)}), f32[16,7,128]{2,1,0:T(8,128)S(1)}, u32[]{:S(2)}, u32[]{:S(2)}) async-start(f32[16,7,128]{2,1,0:T(8,128)} %copy.338), calls=%async_computation.2 | async-start | bytes 131072 | tf_op jit(solution)/shard_map/all_to_all | solution.py:141
  143.0 4.6 collective-permute-start.7
  151.3 8.7 %all-to-all-start.3 = ((f32[16,3,128]{2,1,0:T(4,128)}), f32[16,3,128]{2,1,0:T(4,128)}, u32[]{:S(2)}, u32[]{:S(2)}) async-start(f32[16,3,128]{2,1,0:T(4,128)} %copy.342), calls=%async_computation.3 | async-start | bytes 65536 | tf_op jit(solution)/shard_map/all_to_all | solution.py:152
  168.8 3.7 fusion.96
  180.1 3.8 bitcast_add_fusion.6
  186.9 3.9 multiply_add_fusion.12
  207.2 7.2 %all-to-all-start.4 = ((f32[16,7,128]{2,1,0:T(8,128)}), f32[16,7,128]{2,1,0:T(8,128)S(1)}, u32[]{:S(2)}, u32[]{:S(2)}) async-start(f32[16,7,128]{2,1,0:T(8,128)} %copy.355), calls=%async_computation.4 | async-start | bytes 131072 | tf_op jit(solution)/shard_map/all_to_all | solution.py:141
  222.6 4.6 collective-permute-start.12
  230.9 8.9 %all-to-all-start.5 = ((f32[16,3,128]{2,1,0:T(4,128)}), f32[16,3,128]{2,1,0:T(4,128)}, u32[]{:S(2)}, u32[]{:S(2)}) async-start(f32[16,3,128]{2,1,0:T(4,128)} %copy.359), calls=%async_computation.5 | async-start | bytes 65536 | tf_op jit(solution)/shard_map/all_to_all | solution.py:152
  248.6 3.7 fusion.90
  259.9 3.8 bitcast_add_fusion.5
  266.7 3.9 multiply_add_fusion.10
  287.0 7.2 %all-to-all-start.6 = ((f32[16,7,128]{2,1,0:T(8,128)}), f32[16,7,128]{2,1,0:T(8,128)S(1)}, u32[]{:S(2)}, u32[]{:S(2)}) async-start(f32[16,7,128]{2,1,0:T(8,128)} %copy.372), calls=%async_computation.6 | async-start | bytes 131072 | tf_op jit(solution)/shard_map/all_to_all | solution.py:141
  302.3 4.6 collective-permute-start.17
  310.6 8.7 %all-to-all-start.7 = ((f32[16,3,128]{2,1,0:T(4,128)}), f32[16,3,128]{2,1,0:T(4,128)}, u32[]{:S(2)}, u32[]{:S(2)}) async-start(f32[16,3,128]{2,1,0:T(4,128)} %copy.376), calls=%async_computation.7 | async-start | bytes 65536 | tf_op jit(solution)/shard_map/all_to_all | solution.py:152
  328.0 3.7 fusion.84
  339.3 3.8 bitcast_add_fusion.4
  346.2 3.9 multiply_add_fusion.8
  366.5 7.2 %all-to-all-start.8 = ((f32[16,7,128]{2,1,0:T(8,128)}), f32[16,7,128]{2,1,0:T(8,128)S(1)}, u32[]{:S(2)}, u32[]{:S(2)}) async-start(f32[16,7,128]{2,1,0:T(8,128)} %copy.389), calls=%async_computation.8 | async-start | bytes 131072 | tf_op jit(solution)/shard_map/all_to_all | solution.py:141
  381.8 4.6 collective-permute-start.22
  390.1 8.9 %all-to-all-start.9 = ((f32[16,3,128]{2,1,0:T(4,128)}), f32[16,3,128]{2,1,0:T(4,128)}, u32[]{:S(2)}, u32[]{:S(2)}) async-start(f32[16,3,128]{2,1,0:T(4,128)} %copy.393), calls=%async_computation.9 | async-start | bytes 65536 | tf_op jit(solution)/shard_map/all_to_all | solution.py:152
  407.7 3.7 fusion.78
  419.0 3.8 bitcast_add_fusion.3
  425.8 3.9 multiply_add_fusion.6
  446.1 7.2 %all-to-all-start.10 = ((f32[16,7,128]{2,1,0:T(8,128)}), f32[16,7,128]{2,1,0:T(8,128)S(1)}, u32[]{:S(2)}, u32[]{:S(2)}) async-start(f32[16,7,128]{2,1,0:T(8,128)} %copy.406), calls=%async_computation.10 | async-start | bytes 131072 | tf_op jit(solution)/shard_map/all_to_all | solution.py:141
  461.4 4.6 collective-permute-start.27
  469.7 8.7 %all-to-all-start.11 = ((f32[16,3,128]{2,1,0:T(4,128)}), f32[16,3,128]{2,1,0:T(4,128)}, u32[]{:S(2)}, u32[]{:S(2)}) async-start(f32[16,3,128]{2,1,0:T(4,128)} %copy.410), calls=%async_computation.11 | async-start | bytes 65536 | tf_op jit(solution)/shard_map/all_to_all | solution.py:152
  487.2 3.7 fusion.72
  498.5 3.8 bitcast_add_fusion.2
  505.3 3.9 multiply_add_fusion.4
  525.6 7.2 %all-to-all-start.12 = ((f32[16,7,128]{2,1,0:T(8,128)}), f32[16,7,128]{2,1,0:T(8,128)S(1)}, u32[]{:S(2)}, u32[]{:S(2)}) async-start(f32[16,7,128]{2,1,0:T(8,128)} %copy.423), calls=%async_computation.12 | async-start | bytes 131072 | tf_op jit(solution)/shard_map/all_to_all | solution.py:141
  540.9 4.6 collective-permute-start.32
  549.2 8.9 %all-to-all-start.13 = ((f32[16,3,128]{2,1,0:T(4,128)}), f32[16,3,128]{2,1,0:T(4,128)}, u32[]{:S(2)}, u32[]{:S(2)}) async-start(f32[16,3,128]{2,1,0:T(4,128)} %copy.427), calls=%async_computation.13 | async-start | bytes 65536 | tf_op jit(solution)/shard_map/all_to_all | solution.py:152
  566.5 3.7 fusion.66
  577.8 3.8 bitcast_add_fusion.1
  584.7 3.9 multiply_add_fusion.2
  605.0 7.2 %all-to-all-start.14 = ((f32[16,7,128]{2,1,0:T(8,128)}), f32[16,7,128]{2,1,0:T(8,128)S(1)}, u32[]{:S(2)}, u32[]{:S(2)}) async-start(f32[16,7,128]{2,1,0:T(8,128)} %copy.440), calls=%async_computation.14 | async-start | bytes 131072 | tf_op jit(solution)/shard_map/all_to_all | solution.py:141
  620.2 6.8 %all-to-all-start.15 = ((f32[16,3,128]{2,1,0:T(4,128)}), f32[16,3,128]{2,1,0:T(4,128)S(1)}, u32[]{:S(2)}, u32[]{:S(2)}) async-start(f32[16,3,128]{2,1,0:T(4,128)} %copy.444), calls=%async_computation.15 | async-start | bytes 65536 | tf_op jit(solution)/shard_map/all_to_all | solution.py:152
  627.1 4.6 collective-permute-start.37
  634.9 5.0 collective-permute-done.38
  656.4 4.3 multiply_add_fusion
  (752 shorter events, 395.0 us)
Async XLA Ops:
  26.3 44.1 %all-to-all-start = ((f32[16,7,128]{2,1,0:T(8,128)}), f32[16,7,128]{2,1,0:T(8,128)S(1)}, u32[]{:S(2)}, u32[]{:S(2)}) async-start(f32[16,7,128]{2,1,0:T(8,128)} %copy.319), calls=%async_computation | async-start | bytes 131072 | tf_op jit(solution)/shard_map/all_to_all | solution.py:141
  36.4 22.9 %collective-permute-start.4 = (f32[3,512]{1,0:T(4,128)S(1)}, f32[3,512]{1,0:T(4,128)S(1)}, u32[]{:S(2)}, u32[]{:S(2)}) collective-permute-start(f32[3,512]{1,0:T(4,128)S(1)} %fusion.137), channel_id=1, source_target_pairs={{0,16},{16,0},{32,48},{48,32},{64,80},{80,64},{96,112},{112,96},{1... | collective-permute-start | bytes 18440 | tf_op jit(solution)/shard_map/ppermute | solution.py:33
  36.4 24.9 %collective-permute-start.1 = (f32[3,1,32,128]{3,2,1,0:T(8,128)S(1)}, f32[3,1,32,128]{3,2,1,0:T(8,128)S(1)}, u32[]{:S(2)}, u32[]{:S(2)}) collective-permute-start(f32[3,1,32,128]{3,2,1,0:T(8,128)S(1)} %get-tuple-element.175), channel_id=1, source_target_pairs={{0,16},{16,32},{32,48},{48,64},{64,80},{80,96},{96,112},{1,17},{17... | collective-permute-start | bytes 147464 | tf_op jit(solution)/shard_map/ppermute | solution.py:21
  38.8 22.6 %collective-permute-start = (f32[3,1,32,128]{3,2,1,0:T(8,128)S(1)}, f32[3,1,32,128]{3,2,1,0:T(8,128)S(1)}, u32[]{:S(2)}, u32[]{:S(2)}) collective-permute-start(f32[3,1,32,128]{3,2,1,0:T(8,128)S(1)} %get-tuple-element.174), channel_id=1, source_target_pairs={{16,0},{32,16},{48,32},{64,48},{80,64},{96,80},{112,96},{17,1},{33... | collective-permute-start | bytes 147464 | tf_op jit(solution)/shard_map/ppermute | solution.py:23
  63.4 25.4 %collective-permute-start.2 = (f32[3,34,1,128]{3,2,1,0:T(1,128)}, f32[3,34,1,128]{3,2,1,0:T(1,128)}, u32[]{:S(2)}, u32[]{:S(2)}) collective-permute-start(f32[3,34,1,128]{3,2,1,0:T(1,128)} %get-tuple-element.142), channel_id=1, source_target_pairs={{1,0},{2,1},{3,2},{4,3},{5,4},{6,5},{7,6},{8,7},{9,8},{10,9},{11,1... | collective-permute-start | bytes 156680 | tf_op jit(solution)/shard_map/ppermute | solution.py:23
  68.0 20.8 %collective-permute-start.3 = (f32[3,34,1,128]{3,2,1,0:T(1,128)}, f32[3,34,1,128]{3,2,1,0:T(1,128)}, u32[]{:S(2)}, u32[]{:S(2)}) collective-permute-start(f32[3,34,1,128]{3,2,1,0:T(1,128)} %get-tuple-element.143), channel_id=1, source_target_pairs={{0,1},{1,2},{2,3},{3,4},{4,5},{5,6},{6,7},{7,8},{8,9},{9,10},{10,1... | collective-permute-start | bytes 156680 | tf_op jit(solution)/shard_map/ppermute | solution.py:21
  72.1 14.9 %all-to-all-start.1 = ((f32[16,3,128]{2,1,0:T(4,128)}), f32[16,3,128]{2,1,0:T(4,128)}, u32[]{:S(2)}, u32[]{:S(2)}) async-start(f32[16,3,128]{2,1,0:T(4,128)} %copy.323), calls=%async_computation.1 | async-start | bytes 65536 | tf_op jit(solution)/shard_map/all_to_all | solution.py:152
  125.7 13.3 %collective-permute-start.9 = (f32[3,512]{1,0:T(4,128)S(1)}, f32[3,512]{1,0:T(4,128)S(1)}, u32[]{:S(2)}, u32[]{:S(2)}) collective-permute-start(f32[3,512]{1,0:T(4,128)S(1)} %fusion.38), channel_id=1, source_target_pairs={{0,16},{16,0},{32,48},{48,32},{64,80},{80,64},{96,112},{112,96},{1... | collective-permute-start | bytes 18440 | tf_op jit(solution)/shard_map/ppermute | solution.py:33
  127.4 22.1 %all-to-all-start.2 = ((f32[16,7,128]{2,1,0:T(8,128)}), f32[16,7,128]{2,1,0:T(8,128)S(1)}, u32[]{:S(2)}, u32[]{:S(2)}) async-start(f32[16,7,128]{2,1,0:T(8,128)} %copy.338), calls=%async_computation.2 | async-start | bytes 131072 | tf_op jit(solution)/shard_map/all_to_all | solution.py:141
  143.0 25.8 %collective-permute-start.7 = (f32[3,34,1,128]{3,2,1,0:T(1,128)}, f32[3,34,1,128]{3,2,1,0:T(1,128)}, u32[]{:S(2)}, u32[]{:S(2)}) collective-permute-start(f32[3,34,1,128]{3,2,1,0:T(1,128)} %get-tuple-element.140), channel_id=1, source_target_pairs={{1,0},{2,1},{3,2},{4,3},{5,4},{6,5},{7,6},{8,7},{9,8},{10,9},{11,1... | collective-permute-start | bytes 156680 | tf_op jit(solution)/shard_map/ppermute | solution.py:23
  147.6 21.2 %collective-permute-start.8 = (f32[3,34,1,128]{3,2,1,0:T(1,128)}, f32[3,34,1,128]{3,2,1,0:T(1,128)}, u32[]{:S(2)}, u32[]{:S(2)}) collective-permute-start(f32[3,34,1,128]{3,2,1,0:T(1,128)} %get-tuple-element.141), channel_id=1, source_target_pairs={{0,1},{1,2},{2,3},{3,4},{4,5},{5,6},{6,7},{7,8},{8,9},{9,10},{10,1... | collective-permute-start | bytes 156680 | tf_op jit(solution)/shard_map/ppermute | solution.py:21
  151.3 15.3 %all-to-all-start.3 = ((f32[16,3,128]{2,1,0:T(4,128)}), f32[16,3,128]{2,1,0:T(4,128)}, u32[]{:S(2)}, u32[]{:S(2)}) async-start(f32[16,3,128]{2,1,0:T(4,128)} %copy.342), calls=%async_computation.3 | async-start | bytes 65536 | tf_op jit(solution)/shard_map/all_to_all | solution.py:152
  205.5 13.3 %collective-permute-start.14 = (f32[3,512]{1,0:T(4,128)S(1)}, f32[3,512]{1,0:T(4,128)S(1)}, u32[]{:S(2)}, u32[]{:S(2)}) collective-permute-start(f32[3,512]{1,0:T(4,128)S(1)} %fusion.36), channel_id=1, source_target_pairs={{0,16},{16,0},{32,48},{48,32},{64,80},{80,64},{96,112},{112,96},{1... | collective-permute-start | bytes 18440 | tf_op jit(solution)/shard_map/ppermute | solution.py:33
  207.2 21.9 %all-to-all-start.4 = ((f32[16,7,128]{2,1,0:T(8,128)}), f32[16,7,128]{2,1,0:T(8,128)S(1)}, u32[]{:S(2)}, u32[]{:S(2)}) async-start(f32[16,7,128]{2,1,0:T(8,128)} %copy.355), calls=%async_computation.4 | async-start | bytes 131072 | tf_op jit(solution)/shard_map/all_to_all | solution.py:141
  214.5 6.4 collective-permute-start.10
  222.6 26.0 %collective-permute-start.12 = (f32[3,34,1,128]{3,2,1,0:T(1,128)}, f32[3,34,1,128]{3,2,1,0:T(1,128)}, u32[]{:S(2)}, u32[]{:S(2)}) collective-permute-start(f32[3,34,1,128]{3,2,1,0:T(1,128)} %get-tuple-element.138), channel_id=1, source_target_pairs={{1,0},{2,1},{3,2},{4,3},{5,4},{6,5},{7,6},{8,7},{9,8},{10,9},{11,1... | collective-permute-start | bytes 156680 | tf_op jit(solution)/shard_map/ppermute | solution.py:23
  227.2 21.4 %collective-permute-start.13 = (f32[3,34,1,128]{3,2,1,0:T(1,128)}, f32[3,34,1,128]{3,2,1,0:T(1,128)}, u32[]{:S(2)}, u32[]{:S(2)}) collective-permute-start(f32[3,34,1,128]{3,2,1,0:T(1,128)} %get-tuple-element.139), channel_id=1, source_target_pairs={{0,1},{1,2},{2,3},{3,4},{4,5},{5,6},{6,7},{7,8},{8,9},{9,10},{10,1... | collective-permute-start | bytes 156680 | tf_op jit(solution)/shard_map/ppermute | solution.py:21
  230.9 15.5 %all-to-all-start.5 = ((f32[16,3,128]{2,1,0:T(4,128)}), f32[16,3,128]{2,1,0:T(4,128)}, u32[]{:S(2)}, u32[]{:S(2)}) async-start(f32[16,3,128]{2,1,0:T(4,128)} %copy.359), calls=%async_computation.5 | async-start | bytes 65536 | tf_op jit(solution)/shard_map/all_to_all | solution.py:152
  285.3 13.3 %collective-permute-start.19 = (f32[3,512]{1,0:T(4,128)S(1)}, f32[3,512]{1,0:T(4,128)S(1)}, u32[]{:S(2)}, u32[]{:S(2)}) collective-permute-start(f32[3,512]{1,0:T(4,128)S(1)} %fusion.34), channel_id=1, source_target_pairs={{0,16},{16,0},{32,48},{48,32},{64,80},{80,64},{96,112},{112,96},{1... | collective-permute-start | bytes 18440 | tf_op jit(solution)/shard_map/ppermute | solution.py:33
  287.0 21.8 %all-to-all-start.6 = ((f32[16,7,128]{2,1,0:T(8,128)}), f32[16,7,128]{2,1,0:T(8,128)S(1)}, u32[]{:S(2)}, u32[]{:S(2)}) async-start(f32[16,7,128]{2,1,0:T(8,128)} %copy.372), calls=%async_computation.6 | async-start | bytes 131072 | tf_op jit(solution)/shard_map/all_to_all | solution.py:141
  302.3 25.8 %collective-permute-start.17 = (f32[3,34,1,128]{3,2,1,0:T(1,128)}, f32[3,34,1,128]{3,2,1,0:T(1,128)}, u32[]{:S(2)}, u32[]{:S(2)}) collective-permute-start(f32[3,34,1,128]{3,2,1,0:T(1,128)} %get-tuple-element.136), channel_id=1, source_target_pairs={{1,0},{2,1},{3,2},{4,3},{5,4},{6,5},{7,6},{8,7},{9,8},{10,9},{11,1... | collective-permute-start | bytes 156680 | tf_op jit(solution)/shard_map/ppermute | solution.py:23
  306.9 21.2 %collective-permute-start.18 = (f32[3,34,1,128]{3,2,1,0:T(1,128)}, f32[3,34,1,128]{3,2,1,0:T(1,128)}, u32[]{:S(2)}, u32[]{:S(2)}) collective-permute-start(f32[3,34,1,128]{3,2,1,0:T(1,128)} %get-tuple-element.137), channel_id=1, source_target_pairs={{0,1},{1,2},{2,3},{3,4},{4,5},{5,6},{6,7},{7,8},{8,9},{9,10},{10,1... | collective-permute-start | bytes 156680 | tf_op jit(solution)/shard_map/ppermute | solution.py:21
  310.6 15.3 %all-to-all-start.7 = ((f32[16,3,128]{2,1,0:T(4,128)}), f32[16,3,128]{2,1,0:T(4,128)}, u32[]{:S(2)}, u32[]{:S(2)}) async-start(f32[16,3,128]{2,1,0:T(4,128)} %copy.376), calls=%async_computation.7 | async-start | bytes 65536 | tf_op jit(solution)/shard_map/all_to_all | solution.py:152
  364.8 13.3 %collective-permute-start.24 = (f32[3,512]{1,0:T(4,128)S(1)}, f32[3,512]{1,0:T(4,128)S(1)}, u32[]{:S(2)}, u32[]{:S(2)}) collective-permute-start(f32[3,512]{1,0:T(4,128)S(1)} %fusion.32), channel_id=1, source_target_pairs={{0,16},{16,0},{32,48},{48,32},{64,80},{80,64},{96,112},{112,96},{1... | collective-permute-start | bytes 18440 | tf_op jit(solution)/shard_map/ppermute | solution.py:33
  366.5 21.8 %all-to-all-start.8 = ((f32[16,7,128]{2,1,0:T(8,128)}), f32[16,7,128]{2,1,0:T(8,128)S(1)}, u32[]{:S(2)}, u32[]{:S(2)}) async-start(f32[16,7,128]{2,1,0:T(8,128)} %copy.389), calls=%async_computation.8 | async-start | bytes 131072 | tf_op jit(solution)/shard_map/all_to_all | solution.py:141
  373.7 6.4 collective-permute-start.20
  381.8 25.9 %collective-permute-start.22 = (f32[3,34,1,128]{3,2,1,0:T(1,128)}, f32[3,34,1,128]{3,2,1,0:T(1,128)}, u32[]{:S(2)}, u32[]{:S(2)}) collective-permute-start(f32[3,34,1,128]{3,2,1,0:T(1,128)} %get-tuple-element.134), channel_id=1, source_target_pairs={{1,0},{2,1},{3,2},{4,3},{5,4},{6,5},{7,6},{8,7},{9,8},{10,9},{11,1... | collective-permute-start | bytes 156680 | tf_op jit(solution)/shard_map/ppermute | solution.py:23
  386.3 21.3 %collective-permute-start.23 = (f32[3,34,1,128]{3,2,1,0:T(1,128)}, f32[3,34,1,128]{3,2,1,0:T(1,128)}, u32[]{:S(2)}, u32[]{:S(2)}) collective-permute-start(f32[3,34,1,128]{3,2,1,0:T(1,128)} %get-tuple-element.135), channel_id=1, source_target_pairs={{0,1},{1,2},{2,3},{3,4},{4,5},{5,6},{6,7},{7,8},{8,9},{9,10},{10,1... | collective-permute-start | bytes 156680 | tf_op jit(solution)/shard_map/ppermute | solution.py:21
  390.1 15.5 %all-to-all-start.9 = ((f32[16,3,128]{2,1,0:T(4,128)}), f32[16,3,128]{2,1,0:T(4,128)}, u32[]{:S(2)}, u32[]{:S(2)}) async-start(f32[16,3,128]{2,1,0:T(4,128)} %copy.393), calls=%async_computation.9 | async-start | bytes 65536 | tf_op jit(solution)/shard_map/all_to_all | solution.py:152
  444.4 13.3 %collective-permute-start.29 = (f32[3,512]{1,0:T(4,128)S(1)}, f32[3,512]{1,0:T(4,128)S(1)}, u32[]{:S(2)}, u32[]{:S(2)}) collective-permute-start(f32[3,512]{1,0:T(4,128)S(1)} %fusion.30), channel_id=1, source_target_pairs={{0,16},{16,0},{32,48},{48,32},{64,80},{80,64},{96,112},{112,96},{1... | collective-permute-start | bytes 18440 | tf_op jit(solution)/shard_map/ppermute | solution.py:33
  446.1 21.8 %all-to-all-start.10 = ((f32[16,7,128]{2,1,0:T(8,128)}), f32[16,7,128]{2,1,0:T(8,128)S(1)}, u32[]{:S(2)}, u32[]{:S(2)}) async-start(f32[16,7,128]{2,1,0:T(8,128)} %copy.406), calls=%async_computation.10 | async-start | bytes 131072 | tf_op jit(solution)/shard_map/all_to_all | solution.py:141
  453.4 6.4 collective-permute-start.25
  461.4 25.8 %collective-permute-start.27 = (f32[3,34,1,128]{3,2,1,0:T(1,128)}, f32[3,34,1,128]{3,2,1,0:T(1,128)}, u32[]{:S(2)}, u32[]{:S(2)}) collective-permute-start(f32[3,34,1,128]{3,2,1,0:T(1,128)} %get-tuple-element.132), channel_id=1, source_target_pairs={{1,0},{2,1},{3,2},{4,3},{5,4},{6,5},{7,6},{8,7},{9,8},{10,9},{11,1... | collective-permute-start | bytes 156680 | tf_op jit(solution)/shard_map/ppermute | solution.py:23
  466.0 21.2 %collective-permute-start.28 = (f32[3,34,1,128]{3,2,1,0:T(1,128)}, f32[3,34,1,128]{3,2,1,0:T(1,128)}, u32[]{:S(2)}, u32[]{:S(2)}) collective-permute-start(f32[3,34,1,128]{3,2,1,0:T(1,128)} %get-tuple-element.133), channel_id=1, source_target_pairs={{0,1},{1,2},{2,3},{3,4},{4,5},{5,6},{6,7},{7,8},{8,9},{9,10},{10,1... | collective-permute-start | bytes 156680 | tf_op jit(solution)/shard_map/ppermute | solution.py:21
  469.7 15.3 %all-to-all-start.11 = ((f32[16,3,128]{2,1,0:T(4,128)}), f32[16,3,128]{2,1,0:T(4,128)}, u32[]{:S(2)}, u32[]{:S(2)}) async-start(f32[16,3,128]{2,1,0:T(4,128)} %copy.410), calls=%async_computation.11 | async-start | bytes 65536 | tf_op jit(solution)/shard_map/all_to_all | solution.py:152
  523.9 13.3 %collective-permute-start.34 = (f32[3,512]{1,0:T(4,128)S(1)}, f32[3,512]{1,0:T(4,128)S(1)}, u32[]{:S(2)}, u32[]{:S(2)}) collective-permute-start(f32[3,512]{1,0:T(4,128)S(1)} %fusion.28), channel_id=1, source_target_pairs={{0,16},{16,0},{32,48},{48,32},{64,80},{80,64},{96,112},{112,96},{1... | collective-permute-start | bytes 18440 | tf_op jit(solution)/shard_map/ppermute | solution.py:33
  525.6 21.8 %all-to-all-start.12 = ((f32[16,7,128]{2,1,0:T(8,128)}), f32[16,7,128]{2,1,0:T(8,128)S(1)}, u32[]{:S(2)}, u32[]{:S(2)}) async-start(f32[16,7,128]{2,1,0:T(8,128)} %copy.423), calls=%async_computation.12 | async-start | bytes 131072 | tf_op jit(solution)/shard_map/all_to_all | solution.py:141
  532.8 6.4 collective-permute-start.30
  540.9 25.6 %collective-permute-start.32 = (f32[3,34,1,128]{3,2,1,0:T(1,128)}, f32[3,34,1,128]{3,2,1,0:T(1,128)}, u32[]{:S(2)}, u32[]{:S(2)}) collective-permute-start(f32[3,34,1,128]{3,2,1,0:T(1,128)} %get-tuple-element.130), channel_id=1, source_target_pairs={{1,0},{2,1},{3,2},{4,3},{5,4},{6,5},{7,6},{8,7},{9,8},{10,9},{11,1... | collective-permute-start | bytes 156680 | tf_op jit(solution)/shard_map/ppermute | solution.py:23
  545.5 21.1 %collective-permute-start.33 = (f32[3,34,1,128]{3,2,1,0:T(1,128)}, f32[3,34,1,128]{3,2,1,0:T(1,128)}, u32[]{:S(2)}, u32[]{:S(2)}) collective-permute-start(f32[3,34,1,128]{3,2,1,0:T(1,128)} %get-tuple-element.131), channel_id=1, source_target_pairs={{0,1},{1,2},{2,3},{3,4},{4,5},{5,6},{6,7},{7,8},{8,9},{9,10},{10,1... | collective-permute-start | bytes 156680 | tf_op jit(solution)/shard_map/ppermute | solution.py:21
  549.2 15.2 %all-to-all-start.13 = ((f32[16,3,128]{2,1,0:T(4,128)}), f32[16,3,128]{2,1,0:T(4,128)}, u32[]{:S(2)}, u32[]{:S(2)}) async-start(f32[16,3,128]{2,1,0:T(4,128)} %copy.427), calls=%async_computation.13 | async-start | bytes 65536 | tf_op jit(solution)/shard_map/all_to_all | solution.py:152
  603.3 13.3 %collective-permute-start.39 = (f32[3,512]{1,0:T(4,128)S(1)}, f32[3,512]{1,0:T(4,128)S(1)}, u32[]{:S(2)}, u32[]{:S(2)}) collective-permute-start(f32[3,512]{1,0:T(4,128)S(1)} %fusion.26), channel_id=1, source_target_pairs={{0,16},{16,0},{32,48},{48,32},{64,80},{80,64},{96,112},{112,96},{1... | collective-permute-start | bytes 18440 | tf_op jit(solution)/shard_map/ppermute | solution.py:33
  605.0 13.5 %all-to-all-start.14 = ((f32[16,7,128]{2,1,0:T(8,128)}), f32[16,7,128]{2,1,0:T(8,128)S(1)}, u32[]{:S(2)}, u32[]{:S(2)}) async-start(f32[16,7,128]{2,1,0:T(8,128)} %copy.440), calls=%async_computation.14 | async-start | bytes 131072 | tf_op jit(solution)/shard_map/all_to_all | solution.py:141
  612.2 14.8 %collective-permute-start.35 = (f32[3,1,32,128]{3,2,1,0:T(8,128)S(1)}, f32[3,1,32,128]{3,2,1,0:T(8,128)S(1)}, u32[]{:S(2)}, u32[]{:S(2)}) collective-permute-start(f32[3,1,32,128]{3,2,1,0:T(8,128)S(1)} %get-tuple-element.147), channel_id=1, source_target_pairs={{16,0},{32,16},{48,32},{64,48},{80,64},{96,80},{112,96},{17,1},{33... | collective-permute-start | bytes 147464 | tf_op jit(solution)/shard_map/ppermute | solution.py:23
  614.1 12.9 %collective-permute-start.36 = (f32[3,1,32,128]{3,2,1,0:T(8,128)S(1)}, f32[3,1,32,128]{3,2,1,0:T(8,128)S(1)}, u32[]{:S(2)}, u32[]{:S(2)}) collective-permute-start(f32[3,1,32,128]{3,2,1,0:T(8,128)S(1)} %get-tuple-element.146), channel_id=1, source_target_pairs={{0,16},{16,32},{32,48},{48,64},{64,80},{80,96},{96,112},{1,17},{17... | collective-permute-start | bytes 147464 | tf_op jit(solution)/shard_map/ppermute | solution.py:21
  620.2 13.6 %all-to-all-start.15 = ((f32[16,3,128]{2,1,0:T(4,128)}), f32[16,3,128]{2,1,0:T(4,128)S(1)}, u32[]{:S(2)}, u32[]{:S(2)}) async-start(f32[16,3,128]{2,1,0:T(4,128)} %copy.444), calls=%async_computation.15 | async-start | bytes 65536 | tf_op jit(solution)/shard_map/all_to_all | solution.py:152
  627.1 7.7 %collective-permute-start.37 = (f32[3,34,1,128]{3,2,1,0:T(1,128)S(1)}, f32[3,34,1,128]{3,2,1,0:T(1,128)S(1)}, u32[]{:S(2)}, u32[]{:S(2)}) collective-permute-start(f32[3,34,1,128]{3,2,1,0:T(1,128)S(1)} %get-tuple-element.128), channel_id=1, source_target_pairs={{1,0},{2,1},{3,2},{4,3},{5,4},{6,5},{7,6},{8,7},{9,8},{10,9},{11,1... | collective-permute-start | bytes 156680 | tf_op jit(solution)/shard_map/ppermute | solution.py:23
  631.7 8.1 %collective-permute-start.38 = (f32[3,34,1,128]{3,2,1,0:T(1,128)S(1)}, f32[3,34,1,128]{3,2,1,0:T(1,128)S(1)}, u32[]{:S(2)}, u32[]{:S(2)}) collective-permute-start(f32[3,34,1,128]{3,2,1,0:T(1,128)S(1)} %get-tuple-element.129), channel_id=1, source_target_pairs={{0,1},{1,2},{2,3},{3,4},{4,5},{5,6},{6,7},{7,8},{8,9},{9,10},{10,1... | collective-permute-start | bytes 156680 | tf_op jit(solution)/shard_map/ppermute | solution.py:21
  (117 other events, 469.7 us)
